TPU v7x, 32 devices: a whole 2x2x4 slice. The times are simulated.
32 devices in a mesh: groups: 2 (over y), sec: 4 (over z), strip: 2 (over x), chan: 2 (over core).
Axes of the slice: x: 2, y: 2, z: 4, core: 2. Of those that a mesh axis runs over, the one named last changes fastest.
Arguments:
- sections: bfloat16 [16, 16, 1024], P(('groups', 'sec'), 'strip'), parts along dimension 0, may hold values from -64 to 64
- w_first: bfloat16 [32, 9], replicated, may hold values from -2 to 2
- w_second: bfloat16 [9, 32, 32], replicated, may hold values from -0.375 to 0.375
- offsets: int32 [16, 2, 16, 1024], P(('groups', 'sec'), None, 'strip'), parts along dimension 0, may hold values from -32 to 31
Outputs:
- warped: bfloat16 [16, 32, 16, 1024], P(('groups', 'sec'), 'chan', 'strip'), parts along dimension 0
- composed: float32 [16, 2, 16, 1024], P(('groups', 'sec'), None, 'strip'), parts along dimension 0
There are 2 independent parts, one for each index of `groups`. A program takes and returns all parts, laid end to end along the dimension named above; an argument that names none is the same for every part. Nothing has to cross between parts.
All inputs are finite; a program needn't handle non-finite values.
Results may differ from a plain program's by a relative error of at most 0.0083.
Values may be sent and summed in bfloat16 or wider, within the bound.
No kernel may reach another device: no remote copies, remote signals or barrier semaphores. Data moves between devices by JAX's collectives and lax.ppermute only.
A program may use at most 64 MiB of HBM per device.

v0:
```python
import jax
import jax.numpy as jnp
from jax import lax
from jax.sharding import PartitionSpec as P

score_scale = 4.0


def with_halo(cells, sides, width):
    for axis, dim in sides:
        count = lax.axis_size(axis)
        ends = count - 1
        head = lax.slice_in_dim(cells, 0, width, axis=dim)
        tail = lax.slice_in_dim(cells, cells.shape[dim] - width, cells.shape[dim], axis=dim)
        cells = jnp.concatenate(
            [
                lax.ppermute(tail, axis, [(i, (i + 1) % count) for i in range(ends)]),
                cells,
                lax.ppermute(head, axis, [((i + 1) % count, i) for i in range(ends)]),
            ],
            axis=dim,
        )
    return cells


def from_behind(value, axis, by):
    length = lax.axis_size(axis)
    pairs = [(i, i + by) for i in range(length) if 0 <= i + by < length]
    return lax.ppermute(value, axis, pairs)


def first_taps(extended, rows_out, row_start):
    columns = extended.shape[-1]
    padded = jnp.pad(extended, ((0, 0), (0, 0), (2, 2)))
    tap_list = []
    for shift_y in (-2, 0, 2):
        for shift_x in (-2, 0, 2):
            tap_list.append(
                padded[
                    :,
                    row_start + shift_y : row_start + shift_y + rows_out,
                    2 + shift_x : 2 + shift_x + columns,
                ]
            )
    return jnp.stack(tap_list)


def second_terms(weights, inputs):
    rows_out = inputs.shape[2] - 2
    columns = inputs.shape[3]
    padded = jnp.pad(inputs, ((0, 0), (0, 0), (0, 0), (1, 1)))
    summed = None
    tap_index = 0
    for shift_y in (-1, 0, 1):
        for shift_x in (-1, 0, 1):
            window = padded[
                :, :, 1 + shift_y : 1 + shift_y + rows_out, 1 + shift_x : 1 + shift_x + columns
            ]
            tap_term = jnp.einsum(
                "oi,ispw->ospw", weights[tap_index], window, preferred_element_type=jnp.float32
            )
            summed = tap_term if summed is None else summed + tap_term
            tap_index += 1
    return summed


def hat_weights(quant_row):
    base = jnp.floor_divide(quant_row, 8)
    frac = (quant_row - 8 * base).astype(jnp.float32) * 0.125
    return [
        jnp.where(base == shift, 1.0 - frac, 0.0) + jnp.where(base + 1 == shift, frac, 0.0)
        for shift in range(-4, 5)
    ]


def sample(source, quant, row_start):
    rows_out, columns = (quant.shape[1], quant.shape[2])
    hats_y = hat_weights(quant[0])
    hats_x = hat_weights(quant[1])
    summed = jnp.zeros((source.shape[0], rows_out, columns), jnp.float32)
    for index_x in range(9):
        inner = jnp.zeros((source.shape[0], rows_out, columns), jnp.float32)
        for index_y in range(9):
            lower = row_start + index_y - 4
            window = source[:, lower : lower + rows_out, index_x : index_x + columns].astype(
                jnp.float32
            )
            inner = inner + hats_y[index_y] * window
        summed = summed + hats_x[index_x] * inner
    return summed


def local(sections, w_first, w_second, offsets):
    sec_local, strip_rows, columns = sections.shape
    chan_count = lax.axis_size("chan")
    own_index = lax.axis_index("chan")
    head_width = w_second.shape[1] // chan_count
    strip_first = lax.axis_index("strip") * strip_rows
    total_rows = strip_rows * lax.axis_size("strip")
    extended = with_halo(sections, (("strip", 1),), 3)
    tap_stack = first_taps(extended, strip_rows + 2, 2)
    global_rows = strip_first - 1 + lax.broadcasted_iota(jnp.int32, (strip_rows + 2, 1), 0)
    inside = (global_rows >= 0) & (global_rows < total_rows)
    all_maps = jnp.einsum("ct,tspw->cspw", w_first, tap_stack, preferred_element_type=jnp.float32)
    all_maps = jnp.where(inside, jnp.maximum(all_maps, 0.0), 0.0).astype(jnp.bfloat16)
    w_outputs = lax.dynamic_slice_in_dim(w_second, own_index * head_width, head_width, 1)
    mixed_sum = second_terms(w_outputs, all_maps)
    own_features = jnp.maximum(mixed_sum, 0.0).astype(jnp.bfloat16)
    previous_features = from_behind(own_features[:, sec_local - 1 :], "sec", 1)
    features = jnp.concatenate([previous_features, own_features], axis=1)
    framed = with_halo(features, (("strip", 2),), 4)
    current = framed[:, 1:, 4 : 4 + strip_rows, :]
    earlier = jnp.pad(framed[:, :sec_local], ((0, 0), (0, 0), (0, 0), (4, 4)))
    factor = score_scale / head_width
    field_shape = (sec_local, strip_rows, columns)
    running_max = jnp.full(field_shape, -1e30, jnp.float32)
    weight_sum = jnp.zeros(field_shape, jnp.float32)
    along_y = jnp.zeros(field_shape, jnp.float32)
    along_x = jnp.zeros(field_shape, jnp.float32)
    step_cols = lax.broadcasted_iota(jnp.float32, (9, 1, 1, 1), 0) - 4.0
    for shift_y in range(9):
        scores = (
            jnp.stack(
                [
                    jnp.einsum(
                        "cspw,cspw->spw",
                        current,
                        earlier[:, :, shift_y : shift_y + strip_rows, shift_x : shift_x + columns],
                        preferred_element_type=jnp.float32,
                    )
                    for shift_x in range(9)
                ]
            )
            * factor
        )
        highest = jnp.maximum(running_max, jnp.max(scores, axis=0))
        rescale = jnp.exp(running_max - highest)
        weights = jnp.exp(scores - highest)
        block_sum = jnp.sum(weights, axis=0)
        weight_sum = weight_sum * rescale + block_sum
        along_y = along_y * rescale + (shift_y - 4.0) * block_sum
        along_x = along_x * rescale + jnp.sum(weights * step_cols, axis=0)
        running_max = highest
    head_flow = jnp.stack([along_y / weight_sum, along_x / weight_sum], axis=1)
    flow_field = lax.psum(head_flow.astype(jnp.bfloat16), "chan").astype(jnp.float32) / chan_count
    warped_list = []
    for local_sec in range(sec_local):
        source = jnp.pad(framed[:, local_sec + 1], ((0, 0), (0, 0), (4, 4)))
        warped_list.append(sample(source, offsets[local_sec], 4).astype(jnp.bfloat16))
    warped = jnp.stack(warped_list)
    reach_all = 4 * sec_local
    reach_src = 4 * (sec_local - 1)
    rim_stack = with_halo(
        jnp.concatenate([flow_field, offsets.astype(jnp.float32)], axis=1).astype(jnp.bfloat16),
        (("strip", 2),),
        reach_src,
    ).astype(jnp.float32)
    row_ids = (
        strip_first
        - reach_src
        + lax.broadcasted_iota(jnp.int32, (strip_rows + 2 * reach_src, 1), 0)
    )

    def compose(incoming):
        source = with_halo(incoming.astype(jnp.bfloat16), (("strip", 1),), reach_all).astype(
            incoming.dtype
        )
        results = []
        for local_sec in range(sec_local):
            reach = 4 * (sec_local - 1 - local_sec)
            lower = reach_src - reach
            span = strip_rows + 2 * reach
            portion = rim_stack[local_sec, :, lower : lower + span]
            quant = portion[2:].astype(jnp.int32)
            updated = (
                portion[:2]
                + portion[2:] * 0.125
                + sample(jnp.pad(source, ((0, 0), (0, 0), (4, 4))), quant, 4)
            )
            global_rows = row_ids[lower : lower + span]
            valid_rows = (global_rows >= 0) & (global_rows < total_rows)
            updated = jnp.where(valid_rows, updated, 0.0)
            source = updated
            results.append(updated[:, reach : reach + strip_rows])
        return jnp.stack(results)

    def chain_turn(turn, state_pair):
        incoming = from_behind(state_pair[0].astype(jnp.bfloat16), "sec", 1).astype(jnp.float32)
        composed_all = compose(incoming)
        return (composed_all[sec_local - 1], composed_all)

    start_pair = (
        jnp.zeros((2, strip_rows, columns), jnp.float32),
        jnp.zeros((sec_local, 2, strip_rows, columns), jnp.float32),
    )
    composed = lax.fori_loop(0, lax.axis_size("sec"), chain_turn, start_pair)[1]
    return (warped, composed)


def solution(mesh):
    in_specs = (
        P(("groups", "sec"), "strip", None),
        P(),
        P(),
        P(("groups", "sec"), None, "strip", None),
    )
    out_specs = (
        P(("groups", "sec"), "chan", "strip", None),
        P(("groups", "sec"), None, "strip", None),
    )
    return jax.shard_map(local, mesh=mesh, in_specs=in_specs, out_specs=out_specs, check_vma=False)
```

profile of v0, /device:TPU:10, one launch (start us, length us, event | category | flops | bytes accessed | tf_op | source)
XLA Modules:
  0.0 182.5 jit_solution(9279792757851363367)
XLA Ops:
  8.1 2.4 %collective-permute-start.4 = (bf16[2,3,1024]{2,1,0:T(4,128)(2,1)S(1)}, bf16[2,3,1024]{2,1,0:T(4,128)(2,1)S(1)}, u32[]{:S(2)}, u32[]{:S(2)}) collective-permute-start(bf16[2,3,1024]{2,1,0:T(4,128)(2,1)S(1)} %get-tuple-element.606), channel_id=1, source_target_pairs={{2,0},{3,1},{6,4},{7,5},{10,8},{11,9},{14,12},{15,13},{18,16},{19,... | collective-permute-start | bytes 36872 | tf_op jit(solution)/shard_map/ppermute | solution.py:19
  12.0 4.2 %collective-permute-done.3 = bf16[2,3,1024]{2,1,0:T(4,128)(2,1)S(1)} collective-permute-done((bf16[2,3,1024]{2,1,0:T(4,128)(2,1)S(1)}, bf16[2,3,1024]{2,1,0:T(4,128)(2,1)S(1)}, u32[]{:S(2)}, u32[]{:S(2)}) %collective-permute-start.3) | collective-permute-done | bytes 12320 | tf_op jit(solution)/shard_map/ppermute | solution.py:17
  18.7 2.0 %stack.345 = bf16[9,2,10,1024]{3,0,2,1:T(8,128)(2,1)S(1)} concatenate(bf16[1,2,10,1024]{3,0,2,1:T(2,128)(2,1)S(1)} %copy.208, bf16[1,2,10,1024]{3,0,2,1:T(2,128)(2,1)S(1)} %copy.209, bf16[1,2,10,1024]{3,0,2,1:T(2,128)(2,1)S(1)} %copy.210, bf16[1,2,10,1024]{3,0,2,1:T(2,128)(2,1)S(1)} %copy.211, bf16[1,2,10,1024]{3,0,2,1:T(2,128)(2,1)S(1)} %copy.212, ...), dimensions={0} | concatenate | bytes 737280 | tf_op jit(solution)/shard_map/stack | solution.py:45
  25.1 3.5 %collective-permute-start.5 = (bf16[16,1,8,1024]{3,0,2,1:T(8,128)(2,1)S(1)}, bf16[16,1,8,1024]{3,0,2,1:T(8,128)(2,1)S(1)}, u32[]{:S(2)}, u32[]{:S(2)}) collective-permute-start(bf16[16,1,8,1024]{3,0,2,1:T(8,128)(2,1)S(1)} %slice.2649), channel_id=1, source_target_pairs={{0,4},{4,8},{8,12},{1,5},{5,9},{9,13},{2,6},{6,10},{10,14},{3,7},{... | collective-permute-start | bytes 786440 | tf_op jit(solution)/shard_map/ppermute | solution.py:29
  29.5 4.1 %collective-permute-done.5 = bf16[16,1,8,1024]{3,0,2,1:T(8,128)(2,1)S(1)} collective-permute-done((bf16[16,1,8,1024]{3,0,2,1:T(8,128)(2,1)S(1)}, bf16[16,1,8,1024]{3,0,2,1:T(8,128)(2,1)S(1)}, u32[]{:S(2)}, u32[]{:S(2)}) %collective-permute-start.5) | collective-permute-done | bytes 262176 | tf_op jit(solution)/shard_map/ppermute | solution.py:29
  33.6 2.0 %collective-permute-start.7 = (bf16[16,3,4,1024]{3,0,2,1:T(8,128)(2,1)S(1)}, bf16[16,3,4,1024]{3,0,2,1:T(8,128)(2,1)S(1)}, u32[]{:S(2)}, u32[]{:S(2)}) collective-permute-start(bf16[16,3,4,1024]{3,0,2,1:T(8,128)(2,1)S(1)} %get-tuple-element.544), channel_id=1, source_target_pairs={{2,0},{3,1},{6,4},{7,5},{10,8},{11,9},{14,12},{15,13},{18,16},{19,... | collective-permute-start | bytes 1179656 | tf_op jit(solution)/shard_map/ppermute | solution.py:19
  37.2 4.7 %collective-permute-done.7 = bf16[16,3,4,1024]{3,0,2,1:T(8,128)(2,1)S(1)} collective-permute-done((bf16[16,3,4,1024]{3,0,2,1:T(8,128)(2,1)S(1)}, bf16[16,3,4,1024]{3,0,2,1:T(8,128)(2,1)S(1)}, u32[]{:S(2)}, u32[]{:S(2)}) %collective-permute-start.7) | collective-permute-done | bytes 393248 | tf_op jit(solution)/shard_map/ppermute | solution.py:19
  41.9 4.1 %collective-permute-done.6 = bf16[16,3,4,1024]{3,0,2,1:T(8,128)(2,1)S(1)} collective-permute-done((bf16[16,3,4,1024]{3,0,2,1:T(8,128)(2,1)S(1)}, bf16[16,3,4,1024]{3,0,2,1:T(8,128)(2,1)S(1)}, u32[]{:S(2)}, u32[]{:S(2)}) %collective-permute-start.6) | collective-permute-done | bytes 393248 | tf_op jit(solution)/shard_map/ppermute | solution.py:17
  46.4 3.0 %fusion.345 = (f32[2,8,1024]{2,1,0:T(8,128)S(1)}, f32[2,8,1024]{2,1,0:T(8,128)S(1)}, f32[2,8,1024]{2,1,0:T(8,128)S(1)}, f32[2,8,1024]{2,1,0:T(8,128)S(1)}, f32[2...) fusion(bf16[16,2,8,1024]{3,0,2,1:T(8,128)(2,1)S(1)} %fusion.336, ...), kind=kLoop, calls=%fused_computation.661 | loop fusion | flops 7192576 | bytes 2162688 | tf_op jit(solution)/shard_map/cspw,cspw->spw/dot_general | solution.py:125
  49.4 2.8 %fusion.408 = (f32[2,8,1024]{2,1,0:T(8,128)S(1)}, f32[2,8,1024]{2,1,0:T(8,128)S(1)}, f32[2,8,1024]{2,1,0:T(8,128)S(1)}, f32[2,8,1024]{2,1,0:T(8,128)S(1)}, f32[2...) fusion(bf16[16,2,8,1024]{3,0,2,1:T(8,128)(2,1)S(1)} %fusion.336, ...), kind=kLoop, calls=%fused_computation.724 | loop fusion | flops 7192576 | bytes 2162688 | tf_op jit(solution)/shard_map/cspw,cspw->spw/dot_general | solution.py:125
  52.2 2.7 %fusion.397 = (f32[2,8,1024]{2,1,0:T(8,128)S(1)}, f32[2,8,1024]{2,1,0:T(8,128)S(1)}, f32[2,8,1024]{2,1,0:T(8,128)S(1)}, f32[2,8,1024]{2,1,0:T(8,128)S(1)}, f32[2...) fusion(bf16[16,2,8,1024]{3,0,2,1:T(8,128)(2,1)S(1)} %fusion.336, ...), kind=kLoop, calls=%fused_computation.713 | loop fusion | flops 7192576 | bytes 2162688 | tf_op jit(solution)/shard_map/cspw,cspw->spw/dot_general | solution.py:125
  54.9 2.7 %fusion.407 = (f32[2,8,1024]{2,1,0:T(8,128)S(1)}, f32[2,8,1024]{2,1,0:T(8,128)S(1)}, f32[2,8,1024]{2,1,0:T(8,128)S(1)}, f32[2,8,1024]{2,1,0:T(8,128)S(1)}, f32[2...) fusion(bf16[16,2,8,1024]{3,0,2,1:T(8,128)(2,1)S(1)} %fusion.336, ...), kind=kLoop, calls=%fused_computation.723 | loop fusion | flops 7192576 | bytes 2162688 | tf_op jit(solution)/shard_map/cspw,cspw->spw/dot_general | solution.py:125
  57.6 2.8 %fusion.376 = (f32[2,8,1024]{2,1,0:T(8,128)S(1)}, f32[2,8,1024]{2,1,0:T(8,128)S(1)}, f32[2,8,1024]{2,1,0:T(8,128)S(1)}, f32[2,8,1024]{2,1,0:T(8,128)S(1)}, f32[2...) fusion(bf16[16,2,8,1024]{3,0,2,1:T(8,128)(2,1)S(1)} %fusion.336, ...), kind=kLoop, calls=%fused_computation.692 | loop fusion | flops 7192576 | bytes 2162688 | tf_op jit(solution)/shard_map/cspw,cspw->spw/dot_general | solution.py:125
  60.5 2.8 %fusion.387 = (f32[2,8,1024]{2,1,0:T(8,128)S(1)}, f32[2,8,1024]{2,1,0:T(8,128)S(1)}, f32[2,8,1024]{2,1,0:T(8,128)S(1)}, f32[2,8,1024]{2,1,0:T(8,128)S(1)}, f32[2...) fusion(bf16[16,2,8,1024]{3,0,2,1:T(8,128)(2,1)S(1)} %fusion.336, ...), kind=kLoop, calls=%fused_computation.703 | loop fusion | flops 7192576 | bytes 2162688 | tf_op jit(solution)/shard_map/cspw,cspw->spw/dot_general | solution.py:125
  63.3 2.8 %fusion.356 = (f32[2,8,1024]{2,1,0:T(8,128)S(1)}, f32[2,8,1024]{2,1,0:T(8,128)S(1)}, f32[2,8,1024]{2,1,0:T(8,128)S(1)}, f32[2,8,1024]{2,1,0:T(8,128)S(1)}, f32[2...) fusion(bf16[16,2,8,1024]{3,0,2,1:T(8,128)(2,1)S(1)} %fusion.336, ...), kind=kLoop, calls=%fused_computation.672 | loop fusion | flops 7192576 | bytes 2162688 | tf_op jit(solution)/shard_map/cspw,cspw->spw/dot_general | solution.py:125
  66.0 2.9 %fusion.366 = (f32[2,8,1024]{2,1,0:T(8,128)S(1)}, f32[2,8,1024]{2,1,0:T(8,128)S(1)}, f32[2,8,1024]{2,1,0:T(8,128)S(1)}, f32[2,8,1024]{2,1,0:T(8,128)S(1)}, f32[2...) fusion(bf16[16,2,8,1024]{3,0,2,1:T(8,128)(2,1)S(1)} %fusion.336, ...), kind=kLoop, calls=%fused_computation.682 | loop fusion | flops 7192576 | bytes 2162688 | tf_op jit(solution)/shard_map/cspw,cspw->spw/dot_general | solution.py:125
  69.2 2.1 %fusion.404 = (f32[2,8,1024]{2,1,0:T(8,128)S(1)}, f32[2,8,1024]{2,1,0:T(8,128)S(1)}, f32[2,8,1024]{2,1,0:T(8,128)S(1)}, f32[2,8,1024]{2,1,0:T(8,128)S(1)}, f32[2...) fusion(bf16[16,3,12,1024]{3,0,2,1:T(8,128)(2,1)S(1)} %get-tuple, ...), kind=kLoop, calls=%fused_computation.720 | loop fusion | flops 7454720 | bytes 5570560 | tf_op jit(solution)/shard_map/cspw,cspw->spw/dot_general | solution.py:125
  75.5 7.0 %fusion.447 = bf16[1,16,8,1024]{3,1,2,0:T(8,128)(2,1)S(1)} fusion(f32[8,1024]{1,0:T(8,128)S(1)} %copy-done.10, f32[8,1024]{1,0:T(8,128)S(1)} %get-tuple-element.567, f32[8,1024]{1,0:T(8,128)S(1)} %get-tuple-element.566, f32[8,1024]{1,0:T(8,128)S(1)} %get-tuple-element.565, bf16[16,16,1024]{2,0,1:T(8,128)(2,1)S(1)} %get-tuple-element.540, ...), kind=kLoop, calls=%fused_computation.825 | loop fusion | flops 33030144 | bytes 3735552 | tf_op jit(solution)/shard_map/stack | solution.py:150
  82.6 7.0 %fusion.446 = bf16[1,16,8,1024]{3,1,2,0:T(8,128)(2,1)S(1)} fusion(f32[8,1024]{1,0:T(8,128)S(1)} %copy-done.8, f32[8,1024]{1,0:T(8,128)S(1)} %copy-done.7, f32[8,1024]{1,0:T(8,128)S(1)} %copy-done.6, f32[8,1024]{1,0:T(8,128)S(1)} %copy-done.5, bf16[16,16,1024]{2,0,1:T(8,128)(2,1)S(1)} %get-tuple-element.539, f32[8,1024]{1,0:T(8,128)S(1)} %copy-done.4, ...), kind=kLoop, calls=%fused_computation.824 | loop fusion | flops 33030144 | bytes 3735552 | tf_op jit(solution)/shard_map/stack | solution.py:150
  89.6 5.0 %all-reduce.9.cloned.1.call-done = bf16[2,2,8,1024]{3,2,0,1:T(8,128)(2,1)} async-done(((bf16[2,2,8,1024]{3,2,0,1:T(8,128)(2,1)}), bf16[2,2,8,1024]{3,2,0,1:T(8,128)(2,1)}) %all-reduce.9.cloned.1.call-update) | async-done | bytes 65552 | tf_op jit(solution)/shard_map/psum | solution.py:145
  95.5 2.5 %collective-permute-start.9 = (bf16[2,4,4,1024]{3,2,0,1:T(4,128)(2,1)S(1)}, bf16[2,4,4,1024]{3,2,0,1:T(4,128)(2,1)S(1)}, u32[]{:S(2)}, u32[]{:S(2)}) collective-permute-start(bf16[2,4,4,1024]{3,2,0,1:T(4,128)(2,1)S(1)} %get-tuple-element.554), channel_id=1, source_target_pairs={{2,0},{3,1},{6,4},{7,5},{10,8},{11,9},{14,12},{15,13},{18,16},{19,... | collective-permute-start | bytes 196616 | tf_op jit(solution)/shard_map/ppermute | solution.py:19
  98.0 1.3 collective-permute-start.8
  100.4 3.7 %collective-permute-done.8 = bf16[2,4,4,1024]{3,2,0,1:T(4,128)(2,1)S(1)} collective-permute-done((bf16[2,4,4,1024]{3,2,0,1:T(4,128)(2,1)S(1)}, bf16[2,4,4,1024]{3,2,0,1:T(4,128)(2,1)S(1)}, u32[]{:S(2)}, u32[]{:S(2)}) %collective-permute-start.8) | collective-permute-done | bytes 65568 | tf_op jit(solution)/shard_map/ppermute | solution.py:17
  104.4 71.3 %while.16 = (s32[]{:T(128)}, f32[2,8,1024]{2,1,0:T(8,128)S(1)}, f32[2,2,8,1024]{3,2,1,0:T(8,128)}, s32[16,1]{0,1:T(1,128)S(1)}, f32[2,4,16,1024]{3,2,1,0:T(8,128...) while((s32[]{:T(128)}, f32[2,8,1024]{2,1,0:T(8,128)S(1)}, ...), condition=%wide.region_29.30_spmd.clone, body=%wide.region_28.29_spmd.clone.sunk | while | flops 12337227 | bytes 8586647 | solution.py:196
  104.7 3.4 %collective-permute-start = (bf16[2,8,1024]{2,1,0:T(8,128)(2,1)S(1)}, bf16[2,8,1024]{2,1,0:T(8,128)(2,1)S(1)}, u32[]{:S(2)}, u32[]{:S(2)}) collective-permute-start(bf16[2,8,1024]{2,1,0:T(8,128)(2,1)S(1)} %select_convert_fusion.3), channel_id=1, source_target_pairs={{0,4},{4,8},{8,12},{1,5},{5,9},{9,13},{2,6},{6,10},{10,14},{3,7},{... | collective-permute-start | bytes 98312 | tf_op jit(solution)/shard_map/while/body/eval_jaxpr/ppermute | solution.py:29
  108.6 1.9 %collective-permute-done = bf16[2,8,1024]{2,1,0:T(8,128)(2,1)S(1)} collective-permute-done((bf16[2,8,1024]{2,1,0:T(8,128)(2,1)S(1)}, bf16[2,8,1024]{2,1,0:T(8,128)(2,1)S(1)}, u32[]{:S(2)}, u32[]{:S(2)}) %collective-permute-start) | collective-permute-done | bytes 32800 | tf_op jit(solution)/shard_map/while/body/eval_jaxpr/ppermute | solution.py:29
  110.5 1.6 collective-permute-start.1
  113.6 4.2 %collective-permute-done.2 = bf16[2,8,1024]{2,1,0:T(8,128)(2,1)S(1)} collective-permute-done((bf16[2,8,1024]{2,1,0:T(8,128)(2,1)S(1)}, bf16[2,8,1024]{2,1,0:T(8,128)(2,1)S(1)}, u32[]{:S(2)}, u32[]{:S(2)}) %collective-permute-start.2) | collective-permute-done | bytes 32800 | tf_op jit(solution)/shard_map/while/body/eval_jaxpr/ppermute | solution.py:17
  117.9 2.5 %fusion.537 = f32[2,16,1024]{2,1,0:T(8,128)S(1)} fusion(f32[2,24,1024]{2,1,0:T(8,128)S(1)} %maximum_convert_fusion.3, f32[2,4,16,1024]{3,2,1,0:T(8,128)S(1)} %get-tuple-element.838, f32[16,1024]{1,0:T(8,128)S(1)} %get-tuple-element.762, f32[16,1024]{1,0:T(8,128)S(1)} %get-tuple-element.763, f32[16,1024]{1,0:T(8,128)S(1)} %get-tuple-element.764, ...), kind=kLoop, calls=%fused_computation.244.clone.1 | loop fusion | flops 5701632 | bytes 2949632 | tf_op jit(solution)/shard_map/while/body/eval_jaxpr/jit(_where)/select_n | solution.py:182
  120.4 1.3 fusion.538
  122.4 3.4 %collective-permute-start = (bf16[2,8,1024]{2,1,0:T(8,128)(2,1)S(1)}, bf16[2,8,1024]{2,1,0:T(8,128)(2,1)S(1)}, u32[]{:S(2)}, u32[]{:S(2)}) collective-permute-start(bf16[2,8,1024]{2,1,0:T(8,128)(2,1)S(1)} %select_convert_fusion.3), channel_id=1, source_target_pairs={{0,4},{4,8},{8,12},{1,5},{5,9},{9,13},{2,6},{6,10},{10,14},{3,7},{... | collective-permute-start | bytes 98312 | tf_op jit(solution)/shard_map/while/body/eval_jaxpr/ppermute | solution.py:29
  126.4 1.9 %collective-permute-done = bf16[2,8,1024]{2,1,0:T(8,128)(2,1)S(1)} collective-permute-done((bf16[2,8,1024]{2,1,0:T(8,128)(2,1)S(1)}, bf16[2,8,1024]{2,1,0:T(8,128)(2,1)S(1)}, u32[]{:S(2)}, u32[]{:S(2)}) %collective-permute-start) | collective-permute-done | bytes 32800 | tf_op jit(solution)/shard_map/while/body/eval_jaxpr/ppermute | solution.py:29
  128.2 1.6 collective-permute-start.1
  131.4 4.2 %collective-permute-done.2 = bf16[2,8,1024]{2,1,0:T(8,128)(2,1)S(1)} collective-permute-done((bf16[2,8,1024]{2,1,0:T(8,128)(2,1)S(1)}, bf16[2,8,1024]{2,1,0:T(8,128)(2,1)S(1)}, u32[]{:S(2)}, u32[]{:S(2)}) %collective-permute-start.2) | collective-permute-done | bytes 32800 | tf_op jit(solution)/shard_map/while/body/eval_jaxpr/ppermute | solution.py:17
  135.6 2.5 %fusion.537 = f32[2,16,1024]{2,1,0:T(8,128)S(1)} fusion(f32[2,24,1024]{2,1,0:T(8,128)S(1)} %maximum_convert_fusion.3, f32[2,4,16,1024]{3,2,1,0:T(8,128)S(1)} %get-tuple-element.838, f32[16,1024]{1,0:T(8,128)S(1)} %get-tuple-element.762, f32[16,1024]{1,0:T(8,128)S(1)} %get-tuple-element.763, f32[16,1024]{1,0:T(8,128)S(1)} %get-tuple-element.764, ...), kind=kLoop, calls=%fused_computation.244.clone.1 | loop fusion | flops 5701632 | bytes 2949632 | tf_op jit(solution)/shard_map/while/body/eval_jaxpr/jit(_where)/select_n | solution.py:182
  138.2 1.3 fusion.538
  140.2 3.4 %collective-permute-start = (bf16[2,8,1024]{2,1,0:T(8,128)(2,1)S(1)}, bf16[2,8,1024]{2,1,0:T(8,128)(2,1)S(1)}, u32[]{:S(2)}, u32[]{:S(2)}) collective-permute-start(bf16[2,8,1024]{2,1,0:T(8,128)(2,1)S(1)} %select_convert_fusion.3), channel_id=1, source_target_pairs={{0,4},{4,8},{8,12},{1,5},{5,9},{9,13},{2,6},{6,10},{10,14},{3,7},{... | collective-permute-start | bytes 98312 | tf_op jit(solution)/shard_map/while/body/eval_jaxpr/ppermute | solution.py:29
  144.1 1.9 %collective-permute-done = bf16[2,8,1024]{2,1,0:T(8,128)(2,1)S(1)} collective-permute-done((bf16[2,8,1024]{2,1,0:T(8,128)(2,1)S(1)}, bf16[2,8,1024]{2,1,0:T(8,128)(2,1)S(1)}, u32[]{:S(2)}, u32[]{:S(2)}) %collective-permute-start) | collective-permute-done | bytes 32800 | tf_op jit(solution)/shard_map/while/body/eval_jaxpr/ppermute | solution.py:29
  146.0 1.6 collective-permute-start.1
  149.1 4.2 %collective-permute-done.2 = bf16[2,8,1024]{2,1,0:T(8,128)(2,1)S(1)} collective-permute-done((bf16[2,8,1024]{2,1,0:T(8,128)(2,1)S(1)}, bf16[2,8,1024]{2,1,0:T(8,128)(2,1)S(1)}, u32[]{:S(2)}, u32[]{:S(2)}) %collective-permute-start.2) | collective-permute-done | bytes 32800 | tf_op jit(solution)/shard_map/while/body/eval_jaxpr/ppermute | solution.py:17
  153.4 2.5 %fusion.537 = f32[2,16,1024]{2,1,0:T(8,128)S(1)} fusion(f32[2,24,1024]{2,1,0:T(8,128)S(1)} %maximum_convert_fusion.3, f32[2,4,16,1024]{3,2,1,0:T(8,128)S(1)} %get-tuple-element.838, f32[16,1024]{1,0:T(8,128)S(1)} %get-tuple-element.762, f32[16,1024]{1,0:T(8,128)S(1)} %get-tuple-element.763, f32[16,1024]{1,0:T(8,128)S(1)} %get-tuple-element.764, ...), kind=kLoop, calls=%fused_computation.244.clone.1 | loop fusion | flops 5701632 | bytes 2949632 | tf_op jit(solution)/shard_map/while/body/eval_jaxpr/jit(_where)/select_n | solution.py:182
  155.9 1.3 fusion.538
  157.9 3.4 %collective-permute-start = (bf16[2,8,1024]{2,1,0:T(8,128)(2,1)S(1)}, bf16[2,8,1024]{2,1,0:T(8,128)(2,1)S(1)}, u32[]{:S(2)}, u32[]{:S(2)}) collective-permute-start(bf16[2,8,1024]{2,1,0:T(8,128)(2,1)S(1)} %select_convert_fusion.3), channel_id=1, source_target_pairs={{0,4},{4,8},{8,12},{1,5},{5,9},{9,13},{2,6},{6,10},{10,14},{3,7},{... | collective-permute-start | bytes 98312 | tf_op jit(solution)/shard_map/while/body/eval_jaxpr/ppermute | solution.py:29
  161.9 1.9 %collective-permute-done = bf16[2,8,1024]{2,1,0:T(8,128)(2,1)S(1)} collective-permute-done((bf16[2,8,1024]{2,1,0:T(8,128)(2,1)S(1)}, bf16[2,8,1024]{2,1,0:T(8,128)(2,1)S(1)}, u32[]{:S(2)}, u32[]{:S(2)}) %collective-permute-start) | collective-permute-done | bytes 32800 | tf_op jit(solution)/shard_map/while/body/eval_jaxpr/ppermute | solution.py:29
  163.7 1.6 collective-permute-start.1
  166.9 4.2 %collective-permute-done.2 = bf16[2,8,1024]{2,1,0:T(8,128)(2,1)S(1)} collective-permute-done((bf16[2,8,1024]{2,1,0:T(8,128)(2,1)S(1)}, bf16[2,8,1024]{2,1,0:T(8,128)(2,1)S(1)}, u32[]{:S(2)}, u32[]{:S(2)}) %collective-permute-start.2) | collective-permute-done | bytes 32800 | tf_op jit(solution)/shard_map/while/body/eval_jaxpr/ppermute | solution.py:17
  171.1 2.5 %fusion.537 = f32[2,16,1024]{2,1,0:T(8,128)S(1)} fusion(f32[2,24,1024]{2,1,0:T(8,128)S(1)} %maximum_convert_fusion.3, f32[2,4,16,1024]{3,2,1,0:T(8,128)S(1)} %get-tuple-element.838, f32[16,1024]{1,0:T(8,128)S(1)} %get-tuple-element.762, f32[16,1024]{1,0:T(8,128)S(1)} %get-tuple-element.763, f32[16,1024]{1,0:T(8,128)S(1)} %get-tuple-element.764, ...), kind=kLoop, calls=%fused_computation.244.clone.1 | loop fusion | flops 5701632 | bytes 2949632 | tf_op jit(solution)/shard_map/while/body/eval_jaxpr/jit(_where)/select_n | solution.py:182
  173.7 1.3 fusion.538
  (234 shorter events, 28.8 us)
Async XLA Ops:
  7.2 14.1 %copy-start = (bf16[9,32,32]{2,1,0:T(8,128)(2,1)S(1)}, bf16[9,32,32]{2,1,0:T(8,128)(2,1)}, u32[]{:S(2)}) copy-start(bf16[9,32,32]{2,1,0:T(8,128)(2,1)} %param.8) | copy-start | bytes 55300
  7.2 87.4 %all-reduce.9.cloned.1.call-start = ((), (), s32[]{:S(2)}) async-start(), calls=%async_computation | async-start | bytes 131072 | tf_op jit(solution)/shard_map/psum | solution.py:145
  8.1 3.9 %collective-permute-start.4 = (bf16[2,3,1024]{2,1,0:T(4,128)(2,1)S(1)}, bf16[2,3,1024]{2,1,0:T(4,128)(2,1)S(1)}, u32[]{:S(2)}, u32[]{:S(2)}) collective-permute-start(bf16[2,3,1024]{2,1,0:T(4,128)(2,1)S(1)} %get-tuple-element.606), channel_id=1, source_target_pairs={{2,0},{3,1},{6,4},{7,5},{10,8},{11,9},{14,12},{15,13},{18,16},{19,... | collective-permute-start | bytes 36872 | tf_op jit(solution)/shard_map/ppermute | solution.py:19
  10.5 5.6 %collective-permute-start.3 = (bf16[2,3,1024]{2,1,0:T(4,128)(2,1)S(1)}, bf16[2,3,1024]{2,1,0:T(4,128)(2,1)S(1)}, u32[]{:S(2)}, u32[]{:S(2)}) collective-permute-start(bf16[2,3,1024]{2,1,0:T(4,128)(2,1)S(1)} %get-tuple-element.605), channel_id=1, source_target_pairs={{0,2},{1,3},{4,6},{5,7},{8,10},{9,11},{12,14},{13,15},{16,18},{17,... | collective-permute-start | bytes 36872 | tf_op jit(solution)/shard_map/ppermute | solution.py:17
  18.2 2.5 %copy-start.16 = (bf16[32,9]{0,1:T(8,128)(2,1)S(1)}, bf16[32,9]{0,1:T(8,128)(2,1)}, u32[]{:S(2)}) copy-start(bf16[32,9]{0,1:T(8,128)(2,1)} %param.7) | copy-start | bytes 1732
  24.5 4.0 %copy-start.1 = (s32[2,2,8,1024]{3,2,1,0:T(8,128)S(1)}, s32[2,2,8,1024]{3,2,1,0:T(8,128)}, u32[]{:S(2)}) copy-start(s32[2,2,8,1024]{3,2,1,0:T(8,128)} %param.9) | copy-start | bytes 393220
  25.1 8.5 %collective-permute-start.5 = (bf16[16,1,8,1024]{3,0,2,1:T(8,128)(2,1)S(1)}, bf16[16,1,8,1024]{3,0,2,1:T(8,128)(2,1)S(1)}, u32[]{:S(2)}, u32[]{:S(2)}) collective-permute-start(bf16[16,1,8,1024]{3,0,2,1:T(8,128)(2,1)S(1)} %slice.2649), channel_id=1, source_target_pairs={{0,4},{4,8},{8,12},{1,5},{5,9},{9,13},{2,6},{6,10},{10,14},{3,7},{... | collective-permute-start | bytes 786440 | tf_op jit(solution)/shard_map/ppermute | solution.py:29
  33.6 8.2 %collective-permute-start.7 = (bf16[16,3,4,1024]{3,0,2,1:T(8,128)(2,1)S(1)}, bf16[16,3,4,1024]{3,0,2,1:T(8,128)(2,1)S(1)}, u32[]{:S(2)}, u32[]{:S(2)}) collective-permute-start(bf16[16,3,4,1024]{3,0,2,1:T(8,128)(2,1)S(1)} %get-tuple-element.544), channel_id=1, source_target_pairs={{2,0},{3,1},{6,4},{7,5},{10,8},{11,9},{14,12},{15,13},{18,16},{19,... | collective-permute-start | bytes 1179656 | tf_op jit(solution)/shard_map/ppermute | solution.py:19
  35.6 10.4 %collective-permute-start.6 = (bf16[16,3,4,1024]{3,0,2,1:T(8,128)(2,1)S(1)}, bf16[16,3,4,1024]{3,0,2,1:T(8,128)(2,1)S(1)}, u32[]{:S(2)}, u32[]{:S(2)}) collective-permute-start(bf16[16,3,4,1024]{3,0,2,1:T(8,128)(2,1)S(1)} %get-tuple-element.543), channel_id=1, source_target_pairs={{0,2},{1,3},{4,6},{5,7},{8,10},{9,11},{12,14},{13,15},{16,18},{17,... | collective-permute-start | bytes 1179656 | tf_op jit(solution)/shard_map/ppermute | solution.py:17
  74.4 0.9 copy-start.10
  74.4 0.9 copy-start.11
  74.4 0.9 copy-start.12
  74.5 0.9 copy-start.13
  74.5 0.9 copy-start.14
  74.5 0.9 copy-start.15
  75.4 7.1 %copy-start.2 = (f32[8,1024]{1,0:T(8,128)S(1)}, f32[8,1024]{1,0:T(8,128)}, u32[]{:S(2)}) copy-start(f32[8,1024]{1,0:T(8,128)} %get-tuple-element.577) | copy-start | bytes 98308
  75.4 7.1 %copy-start.3 = (f32[8,1024]{1,0:T(8,128)S(1)}, f32[8,1024]{1,0:T(8,128)}, u32[]{:S(2)}) copy-start(f32[8,1024]{1,0:T(8,128)} %get-tuple-element.578) | copy-start | bytes 98308
  75.4 7.1 %copy-start.4 = (f32[8,1024]{1,0:T(8,128)S(1)}, f32[8,1024]{1,0:T(8,128)}, u32[]{:S(2)}) copy-start(f32[8,1024]{1,0:T(8,128)} %get-tuple-element.579) | copy-start | bytes 98308
  75.4 7.1 %copy-start.5 = (f32[8,1024]{1,0:T(8,128)S(1)}, f32[8,1024]{1,0:T(8,128)}, u32[]{:S(2)}) copy-start(f32[8,1024]{1,0:T(8,128)} %get-tuple-element.580) | copy-start | bytes 98308
  75.4 7.1 %copy-start.6 = (f32[8,1024]{1,0:T(8,128)S(1)}, f32[8,1024]{1,0:T(8,128)}, u32[]{:S(2)}) copy-start(f32[8,1024]{1,0:T(8,128)} %get-tuple-element.581) | copy-start | bytes 98308
  75.4 7.1 %copy-start.7 = (f32[8,1024]{1,0:T(8,128)S(1)}, f32[8,1024]{1,0:T(8,128)}, u32[]{:S(2)}) copy-start(f32[8,1024]{1,0:T(8,128)} %get-tuple-element.582) | copy-start | bytes 98308
  75.5 7.1 %copy-start.8 = (f32[8,1024]{1,0:T(8,128)S(1)}, f32[8,1024]{1,0:T(8,128)}, u32[]{:S(2)}) copy-start(f32[8,1024]{1,0:T(8,128)} %get-tuple-element.583) | copy-start | bytes 98308
  75.5 7.1 %copy-start.9 = (f32[8,1024]{1,0:T(8,128)S(1)}, f32[8,1024]{1,0:T(8,128)}, u32[]{:S(2)}) copy-start(f32[8,1024]{1,0:T(8,128)} %get-tuple-element.584) | copy-start | bytes 98308
  95.5 4.9 %collective-permute-start.9 = (bf16[2,4,4,1024]{3,2,0,1:T(4,128)(2,1)S(1)}, bf16[2,4,4,1024]{3,2,0,1:T(4,128)(2,1)S(1)}, u32[]{:S(2)}, u32[]{:S(2)}) collective-permute-start(bf16[2,4,4,1024]{3,2,0,1:T(4,128)(2,1)S(1)} %get-tuple-element.554), channel_id=1, source_target_pairs={{2,0},{3,1},{6,4},{7,5},{10,8},{11,9},{14,12},{15,13},{18,16},{19,... | collective-permute-start | bytes 196616 | tf_op jit(solution)/shard_map/ppermute | solution.py:19
  98.0 6.2 %collective-permute-start.8 = (bf16[2,4,4,1024]{3,2,0,1:T(4,128)(2,1)S(1)}, bf16[2,4,4,1024]{3,2,0,1:T(4,128)(2,1)S(1)}, u32[]{:S(2)}, u32[]{:S(2)}) collective-permute-start(bf16[2,4,4,1024]{3,2,0,1:T(4,128)(2,1)S(1)} %get-tuple-element.553), channel_id=1, source_target_pairs={{0,2},{1,3},{4,6},{5,7},{8,10},{9,11},{12,14},{13,15},{16,18},{17,... | collective-permute-start | bytes 196616 | tf_op jit(solution)/shard_map/ppermute | solution.py:17
  104.7 5.8 %collective-permute-start = (bf16[2,8,1024]{2,1,0:T(8,128)(2,1)S(1)}, bf16[2,8,1024]{2,1,0:T(8,128)(2,1)S(1)}, u32[]{:S(2)}, u32[]{:S(2)}) collective-permute-start(bf16[2,8,1024]{2,1,0:T(8,128)(2,1)S(1)} %select_convert_fusion.3), channel_id=1, source_target_pairs={{0,4},{4,8},{8,12},{1,5},{5,9},{9,13},{2,6},{6,10},{10,14},{3,7},{... | collective-permute-start | bytes 98312 | tf_op jit(solution)/shard_map/while/body/eval_jaxpr/ppermute | solution.py:29
  110.5 3.1 %collective-permute-start.1 = (bf16[2,8,1024]{2,1,0:T(8,128)(2,1)S(1)}, bf16[2,8,1024]{2,1,0:T(8,128)(2,1)S(1)}, u32[]{:S(2)}, u32[]{:S(2)}) collective-permute-start(bf16[2,8,1024]{2,1,0:T(8,128)(2,1)S(1)} %collective-permute-done), channel_id=1, source_target_pairs={{2,0},{3,1},{6,4},{7,5},{10,8},{11,9},{14,12},{15,13},{18,16},{19,... | collective-permute-start | bytes 98312 | tf_op jit(solution)/shard_map/while/body/eval_jaxpr/ppermute | solution.py:19
  112.1 5.8 %collective-permute-start.2 = (bf16[2,8,1024]{2,1,0:T(8,128)(2,1)S(1)}, bf16[2,8,1024]{2,1,0:T(8,128)(2,1)S(1)}, u32[]{:S(2)}, u32[]{:S(2)}) collective-permute-start(bf16[2,8,1024]{2,1,0:T(8,128)(2,1)S(1)} %collective-permute-done), channel_id=1, source_target_pairs={{0,2},{1,3},{4,6},{5,7},{8,10},{9,11},{12,14},{13,15},{16,18},{17,... | collective-permute-start | bytes 98312 | tf_op jit(solution)/shard_map/while/body/eval_jaxpr/ppermute | solution.py:17
  122.4 5.8 %collective-permute-start = (bf16[2,8,1024]{2,1,0:T(8,128)(2,1)S(1)}, bf16[2,8,1024]{2,1,0:T(8,128)(2,1)S(1)}, u32[]{:S(2)}, u32[]{:S(2)}) collective-permute-start(bf16[2,8,1024]{2,1,0:T(8,128)(2,1)S(1)} %select_convert_fusion.3), channel_id=1, source_target_pairs={{0,4},{4,8},{8,12},{1,5},{5,9},{9,13},{2,6},{6,10},{10,14},{3,7},{... | collective-permute-start | bytes 98312 | tf_op jit(solution)/shard_map/while/body/eval_jaxpr/ppermute | solution.py:29
  128.2 3.2 %collective-permute-start.1 = (bf16[2,8,1024]{2,1,0:T(8,128)(2,1)S(1)}, bf16[2,8,1024]{2,1,0:T(8,128)(2,1)S(1)}, u32[]{:S(2)}, u32[]{:S(2)}) collective-permute-start(bf16[2,8,1024]{2,1,0:T(8,128)(2,1)S(1)} %collective-permute-done), channel_id=1, source_target_pairs={{2,0},{3,1},{6,4},{7,5},{10,8},{11,9},{14,12},{15,13},{18,16},{19,... | collective-permute-start | bytes 98312 | tf_op jit(solution)/shard_map/while/body/eval_jaxpr/ppermute | solution.py:19
  129.8 5.8 %collective-permute-start.2 = (bf16[2,8,1024]{2,1,0:T(8,128)(2,1)S(1)}, bf16[2,8,1024]{2,1,0:T(8,128)(2,1)S(1)}, u32[]{:S(2)}, u32[]{:S(2)}) collective-permute-start(bf16[2,8,1024]{2,1,0:T(8,128)(2,1)S(1)} %collective-permute-done), channel_id=1, source_target_pairs={{0,2},{1,3},{4,6},{5,7},{8,10},{9,11},{12,14},{13,15},{16,18},{17,... | collective-permute-start | bytes 98312 | tf_op jit(solution)/shard_map/while/body/eval_jaxpr/ppermute | solution.py:17
  140.2 5.8 %collective-permute-start = (bf16[2,8,1024]{2,1,0:T(8,128)(2,1)S(1)}, bf16[2,8,1024]{2,1,0:T(8,128)(2,1)S(1)}, u32[]{:S(2)}, u32[]{:S(2)}) collective-permute-start(bf16[2,8,1024]{2,1,0:T(8,128)(2,1)S(1)} %select_convert_fusion.3), channel_id=1, source_target_pairs={{0,4},{4,8},{8,12},{1,5},{5,9},{9,13},{2,6},{6,10},{10,14},{3,7},{... | collective-permute-start | bytes 98312 | tf_op jit(solution)/shard_map/while/body/eval_jaxpr/ppermute | solution.py:29
  146.0 3.2 %collective-permute-start.1 = (bf16[2,8,1024]{2,1,0:T(8,128)(2,1)S(1)}, bf16[2,8,1024]{2,1,0:T(8,128)(2,1)S(1)}, u32[]{:S(2)}, u32[]{:S(2)}) collective-permute-start(bf16[2,8,1024]{2,1,0:T(8,128)(2,1)S(1)} %collective-permute-done), channel_id=1, source_target_pairs={{2,0},{3,1},{6,4},{7,5},{10,8},{11,9},{14,12},{15,13},{18,16},{19,... | collective-permute-start | bytes 98312 | tf_op jit(solution)/shard_map/while/body/eval_jaxpr/ppermute | solution.py:19
  147.6 5.8 %collective-permute-start.2 = (bf16[2,8,1024]{2,1,0:T(8,128)(2,1)S(1)}, bf16[2,8,1024]{2,1,0:T(8,128)(2,1)S(1)}, u32[]{:S(2)}, u32[]{:S(2)}) collective-permute-start(bf16[2,8,1024]{2,1,0:T(8,128)(2,1)S(1)} %collective-permute-done), channel_id=1, source_target_pairs={{0,2},{1,3},{4,6},{5,7},{8,10},{9,11},{12,14},{13,15},{16,18},{17,... | collective-permute-start | bytes 98312 | tf_op jit(solution)/shard_map/while/body/eval_jaxpr/ppermute | solution.py:17
  157.9 5.8 %collective-permute-start = (bf16[2,8,1024]{2,1,0:T(8,128)(2,1)S(1)}, bf16[2,8,1024]{2,1,0:T(8,128)(2,1)S(1)}, u32[]{:S(2)}, u32[]{:S(2)}) collective-permute-start(bf16[2,8,1024]{2,1,0:T(8,128)(2,1)S(1)} %select_convert_fusion.3), channel_id=1, source_target_pairs={{0,4},{4,8},{8,12},{1,5},{5,9},{9,13},{2,6},{6,10},{10,14},{3,7},{... | collective-permute-start | bytes 98312 | tf_op jit(solution)/shard_map/while/body/eval_jaxpr/ppermute | solution.py:29
  163.7 3.2 %collective-permute-start.1 = (bf16[2,8,1024]{2,1,0:T(8,128)(2,1)S(1)}, bf16[2,8,1024]{2,1,0:T(8,128)(2,1)S(1)}, u32[]{:S(2)}, u32[]{:S(2)}) collective-permute-start(bf16[2,8,1024]{2,1,0:T(8,128)(2,1)S(1)} %collective-permute-done), channel_id=1, source_target_pairs={{2,0},{3,1},{6,4},{7,5},{10,8},{11,9},{14,12},{15,13},{18,16},{19,... | collective-permute-start | bytes 98312 | tf_op jit(solution)/shard_map/while/body/eval_jaxpr/ppermute | solution.py:19
  165.3 5.8 %collective-permute-start.2 = (bf16[2,8,1024]{2,1,0:T(8,128)(2,1)S(1)}, bf16[2,8,1024]{2,1,0:T(8,128)(2,1)S(1)}, u32[]{:S(2)}, u32[]{:S(2)}) collective-permute-start(bf16[2,8,1024]{2,1,0:T(8,128)(2,1)S(1)} %collective-permute-done), channel_id=1, source_target_pairs={{0,2},{1,3},{4,6},{5,7},{8,10},{9,11},{12,14},{13,15},{16,18},{17,... | collective-permute-start | bytes 98312 | tf_op jit(solution)/shard_map/while/body/eval_jaxpr/ppermute | solution.py:17
Sparse Core Ops, SparseCore 0:
  75.5 19.0 all-reduce.8
where the time goes:
time: 183 us
  other arithmetic  66.1 us (36%)
  waiting for transfers between devices  51.1 us (28%)
  starting transfers between devices  39.3 us (21%)
  between operations  15.4 us (8%)
  local copies, waits for them, and re-layouts  5.6 us (3%)
  matrix products  4.26 us (2%)
    ppermute x7, waiting for transfers between devices, with_halo(): lax.ppermute(tail, axis, [(i, (i + 1) % count) for i in range(ends)])  29 us
    dot_general x9, other arithmetic, local(): jnp.einsum('cspw,cspw->spw', current, earlier[:, :, shift_y:shift_y + str...  24.6 us
    ppermute x5, starting transfers between devices, from_behind(): return lax.ppermute(value, axis, pairs)  17 us
    select_n x8, other arithmetic, compose(): updated = jnp.where(valid_rows, updated, 0.0)  15.3 us
    another operation x3, other arithmetic, local(): warped = jnp.stack(warped_list)  14 us
    ppermute x7, starting transfers between devices, with_halo(): lax.ppermute(head, axis, [((i + 1) % count, i) for i in range(ends)])  13.2 us
    ppermute x5, waiting for transfers between devices, from_behind(): return lax.ppermute(value, axis, pairs)  11.5 us
    ppermute x7, starting transfers between devices, with_halo(): lax.ppermute(tail, axis, [(i, (i + 1) % count) for i in range(ends)])  9.04 us
  transfers between devices with their start and end apart: 20, of which 19 were waited for; matrix products, arithmetic and copies ran while one was open for 10% of the time, Pallas kernels for 0%

commit v1 on v0

--- a/solution.py
+++ b/solution.py
@@ -142,7 +142,10 @@
         along_x = along_x * rescale + jnp.sum(weights * step_cols, axis=0)
         running_max = highest
     head_flow = jnp.stack([along_y / weight_sum, along_x / weight_sum], axis=1)
-    flow_field = lax.psum(head_flow.astype(jnp.bfloat16), "chan").astype(jnp.float32) / chan_count
+    flow_field = (
+        jnp.sum(lax.all_gather(head_flow.astype(jnp.bfloat16), "chan"), axis=0).astype(jnp.float32)
+        / chan_count
+    )
     warped_list = []
     for local_sec in range(sec_local):
         source = jnp.pad(framed[:, local_sec + 1], ((0, 0), (0, 0), (4, 4)))

time: 183 us -> 163 us (0.89)
  between operations: 15.4 us -> 2.02 us
  waiting for transfers between devices: 51.1 us -> 42.1 us
  starting transfers between devices: 39.3 us -> 41.6 us
  blocking collectives: 0 us -> 1.9 us
    psum x1 -> x0, waiting for transfers between devices: 5.02 us -> none  [local(): lax.psum(head_flow.astype(jnp.bfloat16), 'chan').astype(jnp.float32)]
    ppermute x7, waiting for transfers between devices: 29 us -> 25.3 us  [with_halo(): lax.ppermute(tail, axis, [(i, (i + 1) % count) for i in range(ends)])]
    ppermute x7, starting transfers between devices: 13.2 us -> 15.2 us  [with_halo(): lax.ppermute(head, axis, [((i + 1) % count, i) for i in range(ends)])]
    all_gather x0 -> x1, blocking collectives: none -> 1.9 us  [local(): lax.all_gather(head_flow.astype(jnp.bfloat16), 'chan')]
  transfers between devices with their start and end apart: 20 -> 19, of which waited for: 19 -> 17; matrix products, arithmetic and copies ran while one was open for 10% -> 11% of each run, Pallas kernels for 0% -> 0%
where the time goes in v1:
time: 163 us; the launch traced here: 162 us
  other arithmetic  64.4 us (40%)
  waiting for transfers between devices  42.1 us (26%)
  starting transfers between devices  41.6 us (26%)
  local copies, waits for them, and re-layouts  5.6 us (3%)
  matrix products  4.26 us (3%)
  between operations  2.02 us (1%)
  blocking collectives  1.9 us (1%)
    ppermute x7, waiting for transfers between devices, with_halo(): lax.ppermute(tail, axis, [(i, (i + 1) % count) for i in range(ends)])  25.3 us
    dot_general x9, other arithmetic, local(): jnp.einsum('cspw,cspw->spw', current, earlier[:, :, shift_y:shift_y + str...  24.3 us
    ppermute x5, starting transfers between devices, from_behind(): return lax.ppermute(value, axis, pairs)  17.3 us
    select_n x8, other arithmetic, compose(): updated = jnp.where(valid_rows, updated, 0.0)  15.3 us
    ppermute x7, starting transfers between devices, with_halo(): lax.ppermute(head, axis, [((i + 1) % count, i) for i in range(ends)])  15.2 us
    another operation x3, other arithmetic, local(): warped = jnp.stack(warped_list)  14 us
    ppermute x5, waiting for transfers between devices, from_behind(): return lax.ppermute(value, axis, pairs)  11.2 us
    ppermute x7, starting transfers between devices, with_halo(): lax.ppermute(tail, axis, [(i, (i + 1) % count) for i in range(ends)])  9.04 us
  transfers between devices with their start and end apart: 19, of which 17 were waited for; matrix products, arithmetic and copies ran while one was open for 11% of the time, Pallas kernels for 0%

profile of v1, /device:TPU:10, one launch (start us, length us, event | category | flops | bytes accessed | tf_op | source)
XLA Modules:
  0.0 162.2 jit_solution(11245004049252585559)
XLA Ops:
  1.5 2.4 %collective-permute-start.4 = (bf16[2,3,1024]{2,1,0:T(4,128)(2,1)S(1)}, bf16[2,3,1024]{2,1,0:T(4,128)(2,1)S(1)}, u32[]{:S(2)}, u32[]{:S(2)}) collective-permute-start(bf16[2,3,1024]{2,1,0:T(4,128)(2,1)S(1)} %get-tuple-element.609), channel_id=1, source_target_pairs={{2,0},{3,1},{6,4},{7,5},{10,8},{11,9},{14,12},{15,13},{18,16},{19,... | collective-permute-start | bytes 36872 | tf_op jit(solution)/shard_map/ppermute | solution.py:19
  3.9 1.3 collective-permute-start.3
  5.4 4.2 %collective-permute-done.3 = bf16[2,3,1024]{2,1,0:T(4,128)(2,1)S(1)} collective-permute-done((bf16[2,3,1024]{2,1,0:T(4,128)(2,1)S(1)}, bf16[2,3,1024]{2,1,0:T(4,128)(2,1)S(1)}, u32[]{:S(2)}, u32[]{:S(2)}) %collective-permute-start.3) | collective-permute-done | bytes 12320 | tf_op jit(solution)/shard_map/ppermute | solution.py:17
  12.1 2.0 %stack.348 = bf16[9,2,10,1024]{3,0,2,1:T(8,128)(2,1)S(1)} concatenate(bf16[1,2,10,1024]{3,0,2,1:T(2,128)(2,1)S(1)} %copy.252, bf16[1,2,10,1024]{3,0,2,1:T(2,128)(2,1)S(1)} %copy.253, bf16[1,2,10,1024]{3,0,2,1:T(2,128)(2,1)S(1)} %copy.254, bf16[1,2,10,1024]{3,0,2,1:T(2,128)(2,1)S(1)} %copy.255, bf16[1,2,10,1024]{3,0,2,1:T(2,128)(2,1)S(1)} %copy.256, ...), dimensions={0} | concatenate | bytes 737280 | tf_op jit(solution)/shard_map/stack | solution.py:45
  18.5 3.5 %collective-permute-start.5 = (bf16[16,1,8,1024]{3,0,2,1:T(8,128)(2,1)S(1)}, bf16[16,1,8,1024]{3,0,2,1:T(8,128)(2,1)S(1)}, u32[]{:S(2)}, u32[]{:S(2)}) collective-permute-start(bf16[16,1,8,1024]{3,0,2,1:T(8,128)(2,1)S(1)} %slice.2649), channel_id=1, source_target_pairs={{0,4},{4,8},{8,12},{1,5},{5,9},{9,13},{2,6},{6,10},{10,14},{3,7},{... | collective-permute-start | bytes 786440 | tf_op jit(solution)/shard_map/ppermute | solution.py:29
  22.9 4.1 %collective-permute-done.5 = bf16[16,1,8,1024]{3,0,2,1:T(8,128)(2,1)S(1)} collective-permute-done((bf16[16,1,8,1024]{3,0,2,1:T(8,128)(2,1)S(1)}, bf16[16,1,8,1024]{3,0,2,1:T(8,128)(2,1)S(1)}, u32[]{:S(2)}, u32[]{:S(2)}) %collective-permute-start.5) | collective-permute-done | bytes 262176 | tf_op jit(solution)/shard_map/ppermute | solution.py:29
  27.1 2.0 %collective-permute-start.7 = (bf16[16,3,4,1024]{3,0,2,1:T(8,128)(2,1)S(1)}, bf16[16,3,4,1024]{3,0,2,1:T(8,128)(2,1)S(1)}, u32[]{:S(2)}, u32[]{:S(2)}) collective-permute-start(bf16[16,3,4,1024]{3,0,2,1:T(8,128)(2,1)S(1)} %get-tuple-element.547), channel_id=1, source_target_pairs={{2,0},{3,1},{6,4},{7,5},{10,8},{11,9},{14,12},{15,13},{18,16},{19,... | collective-permute-start | bytes 1179656 | tf_op jit(solution)/shard_map/ppermute | solution.py:19
  29.0 1.3 collective-permute-start.6
  30.6 4.7 %collective-permute-done.7 = bf16[16,3,4,1024]{3,0,2,1:T(8,128)(2,1)S(1)} collective-permute-done((bf16[16,3,4,1024]{3,0,2,1:T(8,128)(2,1)S(1)}, bf16[16,3,4,1024]{3,0,2,1:T(8,128)(2,1)S(1)}, u32[]{:S(2)}, u32[]{:S(2)}) %collective-permute-start.7) | collective-permute-done | bytes 393248 | tf_op jit(solution)/shard_map/ppermute | solution.py:19
  35.3 4.1 %collective-permute-done.6 = bf16[16,3,4,1024]{3,0,2,1:T(8,128)(2,1)S(1)} collective-permute-done((bf16[16,3,4,1024]{3,0,2,1:T(8,128)(2,1)S(1)}, bf16[16,3,4,1024]{3,0,2,1:T(8,128)(2,1)S(1)}, u32[]{:S(2)}, u32[]{:S(2)}) %collective-permute-start.6) | collective-permute-done | bytes 393248 | tf_op jit(solution)/shard_map/ppermute | solution.py:17
  39.8 2.9 %fusion.345 = (f32[2,8,1024]{2,1,0:T(8,128)S(1)}, f32[2,8,1024]{2,1,0:T(8,128)S(1)}, f32[2,8,1024]{2,1,0:T(8,128)S(1)}, f32[2,8,1024]{2,1,0:T(8,128)S(1)}, f32[2...) fusion(bf16[16,2,8,1024]{3,0,2,1:T(8,128)(2,1)S(1)} %fusion.336, ...), kind=kLoop, calls=%fused_computation.661 | loop fusion | flops 7192576 | bytes 2162688 | tf_op jit(solution)/shard_map/cspw,cspw->spw/dot_general | solution.py:125
  42.8 2.8 %fusion.408 = (f32[2,8,1024]{2,1,0:T(8,128)S(1)}, f32[2,8,1024]{2,1,0:T(8,128)S(1)}, f32[2,8,1024]{2,1,0:T(8,128)S(1)}, f32[2,8,1024]{2,1,0:T(8,128)S(1)}, f32[2...) fusion(bf16[16,2,8,1024]{3,0,2,1:T(8,128)(2,1)S(1)} %fusion.336, ...), kind=kLoop, calls=%fused_computation.724 | loop fusion | flops 7192576 | bytes 2162688 | tf_op jit(solution)/shard_map/cspw,cspw->spw/dot_general | solution.py:125
  45.6 2.7 %fusion.397 = (f32[2,8,1024]{2,1,0:T(8,128)S(1)}, f32[2,8,1024]{2,1,0:T(8,128)S(1)}, f32[2,8,1024]{2,1,0:T(8,128)S(1)}, f32[2,8,1024]{2,1,0:T(8,128)S(1)}, f32[2...) fusion(bf16[16,2,8,1024]{3,0,2,1:T(8,128)(2,1)S(1)} %fusion.336, ...), kind=kLoop, calls=%fused_computation.713 | loop fusion | flops 7192576 | bytes 2162688 | tf_op jit(solution)/shard_map/cspw,cspw->spw/dot_general | solution.py:125
  48.3 2.7 %fusion.407 = (f32[2,8,1024]{2,1,0:T(8,128)S(1)}, f32[2,8,1024]{2,1,0:T(8,128)S(1)}, f32[2,8,1024]{2,1,0:T(8,128)S(1)}, f32[2,8,1024]{2,1,0:T(8,128)S(1)}, f32[2...) fusion(bf16[16,2,8,1024]{3,0,2,1:T(8,128)(2,1)S(1)} %fusion.336, ...), kind=kLoop, calls=%fused_computation.723 | loop fusion | flops 7192576 | bytes 2162688 | tf_op jit(solution)/shard_map/cspw,cspw->spw/dot_general | solution.py:125
  50.9 2.8 %fusion.376 = (f32[2,8,1024]{2,1,0:T(8,128)S(1)}, f32[2,8,1024]{2,1,0:T(8,128)S(1)}, f32[2,8,1024]{2,1,0:T(8,128)S(1)}, f32[2,8,1024]{2,1,0:T(8,128)S(1)}, f32[2...) fusion(bf16[16,2,8,1024]{3,0,2,1:T(8,128)(2,1)S(1)} %fusion.336, ...), kind=kLoop, calls=%fused_computation.692 | loop fusion | flops 7192576 | bytes 2162688 | tf_op jit(solution)/shard_map/cspw,cspw->spw/dot_general | solution.py:125
  53.7 2.8 %fusion.387 = (f32[2,8,1024]{2,1,0:T(8,128)S(1)}, f32[2,8,1024]{2,1,0:T(8,128)S(1)}, f32[2,8,1024]{2,1,0:T(8,128)S(1)}, f32[2,8,1024]{2,1,0:T(8,128)S(1)}, f32[2...) fusion(bf16[16,2,8,1024]{3,0,2,1:T(8,128)(2,1)S(1)} %fusion.336, ...), kind=kLoop, calls=%fused_computation.703 | loop fusion | flops 7192576 | bytes 2162688 | tf_op jit(solution)/shard_map/cspw,cspw->spw/dot_general | solution.py:125
  56.5 2.7 %fusion.356 = (f32[2,8,1024]{2,1,0:T(8,128)S(1)}, f32[2,8,1024]{2,1,0:T(8,128)S(1)}, f32[2,8,1024]{2,1,0:T(8,128)S(1)}, f32[2,8,1024]{2,1,0:T(8,128)S(1)}, f32[2...) fusion(bf16[16,2,8,1024]{3,0,2,1:T(8,128)(2,1)S(1)} %fusion.336, ...), kind=kLoop, calls=%fused_computation.672 | loop fusion | flops 7192576 | bytes 2162688 | tf_op jit(solution)/shard_map/cspw,cspw->spw/dot_general | solution.py:125
  59.2 2.9 %fusion.366 = (f32[2,8,1024]{2,1,0:T(8,128)S(1)}, f32[2,8,1024]{2,1,0:T(8,128)S(1)}, f32[2,8,1024]{2,1,0:T(8,128)S(1)}, f32[2,8,1024]{2,1,0:T(8,128)S(1)}, f32[2...) fusion(bf16[16,2,8,1024]{3,0,2,1:T(8,128)(2,1)S(1)} %fusion.336, ...), kind=kLoop, calls=%fused_computation.682 | loop fusion | flops 7192576 | bytes 2162688 | tf_op jit(solution)/shard_map/cspw,cspw->spw/dot_general | solution.py:125
  62.4 2.1 %fusion.404 = (f32[2,8,1024]{2,1,0:T(8,128)S(1)}, f32[2,8,1024]{2,1,0:T(8,128)S(1)}, f32[2,8,1024]{2,1,0:T(8,128)S(1)}, f32[2,8,1024]{2,1,0:T(8,128)S(1)}, f32[2...) fusion(bf16[16,3,12,1024]{3,0,2,1:T(8,128)(2,1)S(1)} %get-tuple, ...), kind=kLoop, calls=%fused_computation.720 | loop fusion | flops 7454720 | bytes 5570560 | tf_op jit(solution)/shard_map/cspw,cspw->spw/dot_general | solution.py:125
  67.9 1.9 %all_gather.4 = bf16[2,2,2,8,1024]{4,3,2,1,0:T(8,128)(2,1)S(1)} all-gather(bf16[1,2,2,8,1024]{4,3,2,1,0:T(8,128)(2,1)S(1)} %copy.261), channel_id=1, replica_groups=mesh['groups'=2,'sec'=4,'strip'=2,'chan'=2] {'chan'}, dimensions={0}, use_global_device_ids=true | all-gather | bytes 196608 | tf_op jit(solution)/shard_map/all_gather | solution.py:146
  69.9 1.5 collective-permute-start.9
  72.8 7.0 %fusion.447 = bf16[1,16,8,1024]{3,1,2,0:T(8,128)(2,1)S(1)} fusion(f32[8,1024]{1,0:T(8,128)S(1)} %copy-done.10, f32[8,1024]{1,0:T(8,128)S(1)} %get-tuple-element.570, f32[8,1024]{1,0:T(8,128)S(1)} %get-tuple-element.569, f32[8,1024]{1,0:T(8,128)S(1)} %get-tuple-element.568, bf16[16,16,1024]{2,0,1:T(8,128)(2,1)S(1)} %get-tuple-element.543, ...), kind=kLoop, calls=%fused_computation.825 | loop fusion | flops 33030144 | bytes 3735552 | tf_op jit(solution)/shard_map/stack | solution.py:153
  79.8 7.0 %fusion.446 = bf16[1,16,8,1024]{3,1,2,0:T(8,128)(2,1)S(1)} fusion(f32[8,1024]{1,0:T(8,128)S(1)} %copy-done.8, f32[8,1024]{1,0:T(8,128)S(1)} %copy-done.7, f32[8,1024]{1,0:T(8,128)S(1)} %copy-done.6, f32[8,1024]{1,0:T(8,128)S(1)} %copy-done.5, bf16[16,16,1024]{2,0,1:T(8,128)(2,1)S(1)} %get-tuple-element.542, f32[8,1024]{1,0:T(8,128)S(1)} %copy-done.4, ...), kind=kLoop, calls=%fused_computation.824 | loop fusion | flops 33030144 | bytes 3735552 | tf_op jit(solution)/shard_map/stack | solution.py:153
  88.2 74.0 %while.16 = (s32[]{:T(128)}, f32[2,8,1024]{2,1,0:T(8,128)S(1)}, f32[2,2,8,1024]{3,2,1,0:T(8,128)}, s32[16,1]{0,1:T(1,128)S(1)}, f32[2,4,16,1024]{3,2,1,0:T(8,128...) while((s32[]{:T(128)}, f32[2,8,1024]{2,1,0:T(8,128)S(1)}, ...), condition=%wide.region_29.30_spmd.clone, body=%wide.region_28.29_spmd.clone.sunk | while | flops 12337227 | bytes 8586647 | solution.py:199
  88.2 3.5 %collective-permute-start = (bf16[2,8,1024]{2,1,0:T(8,128)(2,1)S(1)}, bf16[2,8,1024]{2,1,0:T(8,128)(2,1)S(1)}, u32[]{:S(2)}, u32[]{:S(2)}) collective-permute-start(bf16[2,8,1024]{2,1,0:T(8,128)(2,1)S(1)} %select_convert_fusion.3), channel_id=1, source_target_pairs={{0,4},{4,8},{8,12},{1,5},{5,9},{9,13},{2,6},{6,10},{10,14},{3,7},{... | collective-permute-start | bytes 98312 | tf_op jit(solution)/shard_map/while/body/eval_jaxpr/ppermute | solution.py:29
  92.3 1.8 %collective-permute-done = bf16[2,8,1024]{2,1,0:T(8,128)(2,1)S(1)} collective-permute-done((bf16[2,8,1024]{2,1,0:T(8,128)(2,1)S(1)}, bf16[2,8,1024]{2,1,0:T(8,128)(2,1)S(1)}, u32[]{:S(2)}, u32[]{:S(2)}) %collective-permute-start) | collective-permute-done | bytes 32800 | tf_op jit(solution)/shard_map/while/body/eval_jaxpr/ppermute | solution.py:29
  94.0 4.5 %collective-permute-start.1 = (bf16[2,8,1024]{2,1,0:T(8,128)(2,1)S(1)}, bf16[2,8,1024]{2,1,0:T(8,128)(2,1)S(1)}, u32[]{:S(2)}, u32[]{:S(2)}) collective-permute-start(bf16[2,8,1024]{2,1,0:T(8,128)(2,1)S(1)} %collective-permute-done), channel_id=1, source_target_pairs={{2,0},{3,1},{6,4},{7,5},{10,8},{11,9},{14,12},{15,13},{18,16},{19,... | collective-permute-start | bytes 98312 | tf_op jit(solution)/shard_map/while/body/eval_jaxpr/ppermute | solution.py:19
  100.2 4.2 %collective-permute-done.2 = bf16[2,8,1024]{2,1,0:T(8,128)(2,1)S(1)} collective-permute-done((bf16[2,8,1024]{2,1,0:T(8,128)(2,1)S(1)}, bf16[2,8,1024]{2,1,0:T(8,128)(2,1)S(1)}, u32[]{:S(2)}, u32[]{:S(2)}) %collective-permute-start.2) | collective-permute-done | bytes 32800 | tf_op jit(solution)/shard_map/while/body/eval_jaxpr/ppermute | solution.py:17
  104.4 2.5 %fusion.538 = f32[2,16,1024]{2,1,0:T(8,128)S(1)} fusion(f32[2,24,1024]{2,1,0:T(8,128)S(1)} %maximum_convert_fusion.3, f32[2,4,16,1024]{3,2,1,0:T(8,128)S(1)} %get-tuple-element.825, f32[16,1024]{1,0:T(8,128)S(1)} %get-tuple-element.749, f32[16,1024]{1,0:T(8,128)S(1)} %get-tuple-element.750, f32[16,1024]{1,0:T(8,128)S(1)} %get-tuple-element.751, ...), kind=kLoop, calls=%fused_computation.244.clone.1 | loop fusion | flops 5701632 | bytes 2949632 | tf_op jit(solution)/shard_map/while/body/eval_jaxpr/jit(_where)/select_n | solution.py:185
  107.0 1.3 fusion.539
  108.9 3.5 %collective-permute-start = (bf16[2,8,1024]{2,1,0:T(8,128)(2,1)S(1)}, bf16[2,8,1024]{2,1,0:T(8,128)(2,1)S(1)}, u32[]{:S(2)}, u32[]{:S(2)}) collective-permute-start(bf16[2,8,1024]{2,1,0:T(8,128)(2,1)S(1)} %select_convert_fusion.3), channel_id=1, source_target_pairs={{0,4},{4,8},{8,12},{1,5},{5,9},{9,13},{2,6},{6,10},{10,14},{3,7},{... | collective-permute-start | bytes 98312 | tf_op jit(solution)/shard_map/while/body/eval_jaxpr/ppermute | solution.py:29
  113.0 1.8 %collective-permute-done = bf16[2,8,1024]{2,1,0:T(8,128)(2,1)S(1)} collective-permute-done((bf16[2,8,1024]{2,1,0:T(8,128)(2,1)S(1)}, bf16[2,8,1024]{2,1,0:T(8,128)(2,1)S(1)}, u32[]{:S(2)}, u32[]{:S(2)}) %collective-permute-start) | collective-permute-done | bytes 32800 | tf_op jit(solution)/shard_map/while/body/eval_jaxpr/ppermute | solution.py:29
  114.7 1.6 collective-permute-start.1
  117.9 4.2 %collective-permute-done.2 = bf16[2,8,1024]{2,1,0:T(8,128)(2,1)S(1)} collective-permute-done((bf16[2,8,1024]{2,1,0:T(8,128)(2,1)S(1)}, bf16[2,8,1024]{2,1,0:T(8,128)(2,1)S(1)}, u32[]{:S(2)}, u32[]{:S(2)}) %collective-permute-start.2) | collective-permute-done | bytes 32800 | tf_op jit(solution)/shard_map/while/body/eval_jaxpr/ppermute | solution.py:17
  122.2 2.5 %fusion.538 = f32[2,16,1024]{2,1,0:T(8,128)S(1)} fusion(f32[2,24,1024]{2,1,0:T(8,128)S(1)} %maximum_convert_fusion.3, f32[2,4,16,1024]{3,2,1,0:T(8,128)S(1)} %get-tuple-element.825, f32[16,1024]{1,0:T(8,128)S(1)} %get-tuple-element.749, f32[16,1024]{1,0:T(8,128)S(1)} %get-tuple-element.750, f32[16,1024]{1,0:T(8,128)S(1)} %get-tuple-element.751, ...), kind=kLoop, calls=%fused_computation.244.clone.1 | loop fusion | flops 5701632 | bytes 2949632 | tf_op jit(solution)/shard_map/while/body/eval_jaxpr/jit(_where)/select_n | solution.py:185
  124.7 1.3 fusion.539
  126.7 3.5 %collective-permute-start = (bf16[2,8,1024]{2,1,0:T(8,128)(2,1)S(1)}, bf16[2,8,1024]{2,1,0:T(8,128)(2,1)S(1)}, u32[]{:S(2)}, u32[]{:S(2)}) collective-permute-start(bf16[2,8,1024]{2,1,0:T(8,128)(2,1)S(1)} %select_convert_fusion.3), channel_id=1, source_target_pairs={{0,4},{4,8},{8,12},{1,5},{5,9},{9,13},{2,6},{6,10},{10,14},{3,7},{... | collective-permute-start | bytes 98312 | tf_op jit(solution)/shard_map/while/body/eval_jaxpr/ppermute | solution.py:29
  130.7 1.8 %collective-permute-done = bf16[2,8,1024]{2,1,0:T(8,128)(2,1)S(1)} collective-permute-done((bf16[2,8,1024]{2,1,0:T(8,128)(2,1)S(1)}, bf16[2,8,1024]{2,1,0:T(8,128)(2,1)S(1)}, u32[]{:S(2)}, u32[]{:S(2)}) %collective-permute-start) | collective-permute-done | bytes 32800 | tf_op jit(solution)/shard_map/while/body/eval_jaxpr/ppermute | solution.py:29
  132.5 1.6 collective-permute-start.1
  135.7 4.2 %collective-permute-done.2 = bf16[2,8,1024]{2,1,0:T(8,128)(2,1)S(1)} collective-permute-done((bf16[2,8,1024]{2,1,0:T(8,128)(2,1)S(1)}, bf16[2,8,1024]{2,1,0:T(8,128)(2,1)S(1)}, u32[]{:S(2)}, u32[]{:S(2)}) %collective-permute-start.2) | collective-permute-done | bytes 32800 | tf_op jit(solution)/shard_map/while/body/eval_jaxpr/ppermute | solution.py:17
  139.9 2.5 %fusion.538 = f32[2,16,1024]{2,1,0:T(8,128)S(1)} fusion(f32[2,24,1024]{2,1,0:T(8,128)S(1)} %maximum_convert_fusion.3, f32[2,4,16,1024]{3,2,1,0:T(8,128)S(1)} %get-tuple-element.825, f32[16,1024]{1,0:T(8,128)S(1)} %get-tuple-element.749, f32[16,1024]{1,0:T(8,128)S(1)} %get-tuple-element.750, f32[16,1024]{1,0:T(8,128)S(1)} %get-tuple-element.751, ...), kind=kLoop, calls=%fused_computation.244.clone.1 | loop fusion | flops 5701632 | bytes 2949632 | tf_op jit(solution)/shard_map/while/body/eval_jaxpr/jit(_where)/select_n | solution.py:185
  142.5 1.3 fusion.539
  144.4 3.5 %collective-permute-start = (bf16[2,8,1024]{2,1,0:T(8,128)(2,1)S(1)}, bf16[2,8,1024]{2,1,0:T(8,128)(2,1)S(1)}, u32[]{:S(2)}, u32[]{:S(2)}) collective-permute-start(bf16[2,8,1024]{2,1,0:T(8,128)(2,1)S(1)} %select_convert_fusion.3), channel_id=1, source_target_pairs={{0,4},{4,8},{8,12},{1,5},{5,9},{9,13},{2,6},{6,10},{10,14},{3,7},{... | collective-permute-start | bytes 98312 | tf_op jit(solution)/shard_map/while/body/eval_jaxpr/ppermute | solution.py:29
  148.5 1.8 %collective-permute-done = bf16[2,8,1024]{2,1,0:T(8,128)(2,1)S(1)} collective-permute-done((bf16[2,8,1024]{2,1,0:T(8,128)(2,1)S(1)}, bf16[2,8,1024]{2,1,0:T(8,128)(2,1)S(1)}, u32[]{:S(2)}, u32[]{:S(2)}) %collective-permute-start) | collective-permute-done | bytes 32800 | tf_op jit(solution)/shard_map/while/body/eval_jaxpr/ppermute | solution.py:29
  150.2 1.6 collective-permute-start.1
  153.4 4.2 %collective-permute-done.2 = bf16[2,8,1024]{2,1,0:T(8,128)(2,1)S(1)} collective-permute-done((bf16[2,8,1024]{2,1,0:T(8,128)(2,1)S(1)}, bf16[2,8,1024]{2,1,0:T(8,128)(2,1)S(1)}, u32[]{:S(2)}, u32[]{:S(2)}) %collective-permute-start.2) | collective-permute-done | bytes 32800 | tf_op jit(solution)/shard_map/while/body/eval_jaxpr/ppermute | solution.py:17
  157.7 2.5 %fusion.538 = f32[2,16,1024]{2,1,0:T(8,128)S(1)} fusion(f32[2,24,1024]{2,1,0:T(8,128)S(1)} %maximum_convert_fusion.3, f32[2,4,16,1024]{3,2,1,0:T(8,128)S(1)} %get-tuple-element.825, f32[16,1024]{1,0:T(8,128)S(1)} %get-tuple-element.749, f32[16,1024]{1,0:T(8,128)S(1)} %get-tuple-element.750, f32[16,1024]{1,0:T(8,128)S(1)} %get-tuple-element.751, ...), kind=kLoop, calls=%fused_computation.244.clone.1 | loop fusion | flops 5701632 | bytes 2949632 | tf_op jit(solution)/shard_map/while/body/eval_jaxpr/jit(_where)/select_n | solution.py:185
  160.2 1.3 fusion.539
  (233 shorter events, 26.0 us)
Async XLA Ops:
  0.6 14.1 %copy-start = (bf16[9,32,32]{2,1,0:T(8,128)(2,1)S(1)}, bf16[9,32,32]{2,1,0:T(8,128)(2,1)}, u32[]{:S(2)}) copy-start(bf16[9,32,32]{2,1,0:T(8,128)(2,1)} %param.8) | copy-start | bytes 55300
  1.5 3.9 %collective-permute-start.4 = (bf16[2,3,1024]{2,1,0:T(4,128)(2,1)S(1)}, bf16[2,3,1024]{2,1,0:T(4,128)(2,1)S(1)}, u32[]{:S(2)}, u32[]{:S(2)}) collective-permute-start(bf16[2,3,1024]{2,1,0:T(4,128)(2,1)S(1)} %get-tuple-element.609), channel_id=1, source_target_pairs={{2,0},{3,1},{6,4},{7,5},{10,8},{11,9},{14,12},{15,13},{18,16},{19,... | collective-permute-start | bytes 36872 | tf_op jit(solution)/shard_map/ppermute | solution.py:19
  3.9 5.6 %collective-permute-start.3 = (bf16[2,3,1024]{2,1,0:T(4,128)(2,1)S(1)}, bf16[2,3,1024]{2,1,0:T(4,128)(2,1)S(1)}, u32[]{:S(2)}, u32[]{:S(2)}) collective-permute-start(bf16[2,3,1024]{2,1,0:T(4,128)(2,1)S(1)} %get-tuple-element.608), channel_id=1, source_target_pairs={{0,2},{1,3},{4,6},{5,7},{8,10},{9,11},{12,14},{13,15},{16,18},{17,... | collective-permute-start | bytes 36872 | tf_op jit(solution)/shard_map/ppermute | solution.py:17
  11.7 2.5 %copy-start.16 = (bf16[32,9]{0,1:T(8,128)(2,1)S(1)}, bf16[32,9]{0,1:T(8,128)(2,1)}, u32[]{:S(2)}) copy-start(bf16[32,9]{0,1:T(8,128)(2,1)} %param.7) | copy-start | bytes 1732
  18.0 4.0 %copy-start.1 = (s32[2,2,8,1024]{3,2,1,0:T(8,128)S(1)}, s32[2,2,8,1024]{3,2,1,0:T(8,128)}, u32[]{:S(2)}) copy-start(s32[2,2,8,1024]{3,2,1,0:T(8,128)} %param.9) | copy-start | bytes 393220
  18.5 8.5 %collective-permute-start.5 = (bf16[16,1,8,1024]{3,0,2,1:T(8,128)(2,1)S(1)}, bf16[16,1,8,1024]{3,0,2,1:T(8,128)(2,1)S(1)}, u32[]{:S(2)}, u32[]{:S(2)}) collective-permute-start(bf16[16,1,8,1024]{3,0,2,1:T(8,128)(2,1)S(1)} %slice.2649), channel_id=1, source_target_pairs={{0,4},{4,8},{8,12},{1,5},{5,9},{9,13},{2,6},{6,10},{10,14},{3,7},{... | collective-permute-start | bytes 786440 | tf_op jit(solution)/shard_map/ppermute | solution.py:29
  27.1 8.2 %collective-permute-start.7 = (bf16[16,3,4,1024]{3,0,2,1:T(8,128)(2,1)S(1)}, bf16[16,3,4,1024]{3,0,2,1:T(8,128)(2,1)S(1)}, u32[]{:S(2)}, u32[]{:S(2)}) collective-permute-start(bf16[16,3,4,1024]{3,0,2,1:T(8,128)(2,1)S(1)} %get-tuple-element.547), channel_id=1, source_target_pairs={{2,0},{3,1},{6,4},{7,5},{10,8},{11,9},{14,12},{15,13},{18,16},{19,... | collective-permute-start | bytes 1179656 | tf_op jit(solution)/shard_map/ppermute | solution.py:19
  29.0 10.4 %collective-permute-start.6 = (bf16[16,3,4,1024]{3,0,2,1:T(8,128)(2,1)S(1)}, bf16[16,3,4,1024]{3,0,2,1:T(8,128)(2,1)S(1)}, u32[]{:S(2)}, u32[]{:S(2)}) collective-permute-start(bf16[16,3,4,1024]{3,0,2,1:T(8,128)(2,1)S(1)} %get-tuple-element.546), channel_id=1, source_target_pairs={{0,2},{1,3},{4,6},{5,7},{8,10},{9,11},{12,14},{13,15},{16,18},{17,... | collective-permute-start | bytes 1179656 | tf_op jit(solution)/shard_map/ppermute | solution.py:17
  67.6 5.1 %copy-start.10 = (f32[8,1024]{1,0:T(8,128)S(1)}, f32[8,1024]{1,0:T(8,128)}, u32[]{:S(2)}) copy-start(f32[8,1024]{1,0:T(8,128)} %get-tuple-element.588) | copy-start | bytes 98308
  67.6 5.1 %copy-start.11 = (f32[8,1024]{1,0:T(8,128)S(1)}, f32[8,1024]{1,0:T(8,128)}, u32[]{:S(2)}) copy-start(f32[8,1024]{1,0:T(8,128)} %get-tuple-element.589) | copy-start | bytes 98308
  67.6 5.1 %copy-start.12 = (f32[8,1024]{1,0:T(8,128)S(1)}, f32[8,1024]{1,0:T(8,128)}, u32[]{:S(2)}) copy-start(f32[8,1024]{1,0:T(8,128)} %get-tuple-element.590) | copy-start | bytes 98308
  67.6 5.1 %copy-start.13 = (f32[8,1024]{1,0:T(8,128)S(1)}, f32[8,1024]{1,0:T(8,128)}, u32[]{:S(2)}) copy-start(f32[8,1024]{1,0:T(8,128)} %get-tuple-element.591) | copy-start | bytes 98308
  67.6 5.1 %copy-start.14 = (f32[8,1024]{1,0:T(8,128)S(1)}, f32[8,1024]{1,0:T(8,128)}, u32[]{:S(2)}) copy-start(f32[8,1024]{1,0:T(8,128)} %get-tuple-element.592) | copy-start | bytes 98308
  67.6 5.1 %copy-start.15 = (f32[8,1024]{1,0:T(8,128)S(1)}, f32[8,1024]{1,0:T(8,128)}, u32[]{:S(2)}) copy-start(f32[8,1024]{1,0:T(8,128)} %get-tuple-element.593) | copy-start | bytes 98308
  69.9 18.1 %collective-permute-start.9 = (bf16[2,4,4,1024]{3,2,1,0:T(4,128)(2,1)S(1)}, bf16[2,4,4,1024]{3,2,1,0:T(4,128)(2,1)S(1)}, u32[]{:S(2)}, u32[]{:S(2)}) collective-permute-start(bf16[2,4,4,1024]{3,2,1,0:T(4,128)(2,1)S(1)} %get-tuple-element.557), channel_id=1, source_target_pairs={{2,0},{3,1},{6,4},{7,5},{10,8},{11,9},{14,12},{15,13},{18,16},{19,... | collective-permute-start | bytes 196616 | tf_op jit(solution)/shard_map/ppermute | solution.py:19
  71.3 16.6 %collective-permute-start.8 = (bf16[2,4,4,1024]{3,2,1,0:T(4,128)(2,1)S(1)}, bf16[2,4,4,1024]{3,2,1,0:T(4,128)(2,1)S(1)}, u32[]{:S(2)}, u32[]{:S(2)}) collective-permute-start(bf16[2,4,4,1024]{3,2,1,0:T(4,128)(2,1)S(1)} %get-tuple-element.556), channel_id=1, source_target_pairs={{0,2},{1,3},{4,6},{5,7},{8,10},{9,11},{12,14},{13,15},{16,18},{17,... | collective-permute-start | bytes 196616 | tf_op jit(solution)/shard_map/ppermute | solution.py:17
  72.7 7.1 %copy-start.2 = (f32[8,1024]{1,0:T(8,128)S(1)}, f32[8,1024]{1,0:T(8,128)}, u32[]{:S(2)}) copy-start(f32[8,1024]{1,0:T(8,128)} %get-tuple-element.580) | copy-start | bytes 98308
  72.7 7.1 %copy-start.3 = (f32[8,1024]{1,0:T(8,128)S(1)}, f32[8,1024]{1,0:T(8,128)}, u32[]{:S(2)}) copy-start(f32[8,1024]{1,0:T(8,128)} %get-tuple-element.581) | copy-start | bytes 98308
  72.7 7.1 %copy-start.4 = (f32[8,1024]{1,0:T(8,128)S(1)}, f32[8,1024]{1,0:T(8,128)}, u32[]{:S(2)}) copy-start(f32[8,1024]{1,0:T(8,128)} %get-tuple-element.582) | copy-start | bytes 98308
  72.7 7.1 %copy-start.5 = (f32[8,1024]{1,0:T(8,128)S(1)}, f32[8,1024]{1,0:T(8,128)}, u32[]{:S(2)}) copy-start(f32[8,1024]{1,0:T(8,128)} %get-tuple-element.583) | copy-start | bytes 98308
  72.7 7.1 %copy-start.6 = (f32[8,1024]{1,0:T(8,128)S(1)}, f32[8,1024]{1,0:T(8,128)}, u32[]{:S(2)}) copy-start(f32[8,1024]{1,0:T(8,128)} %get-tuple-element.584) | copy-start | bytes 98308
  72.7 7.1 %copy-start.7 = (f32[8,1024]{1,0:T(8,128)S(1)}, f32[8,1024]{1,0:T(8,128)}, u32[]{:S(2)}) copy-start(f32[8,1024]{1,0:T(8,128)} %get-tuple-element.585) | copy-start | bytes 98308
  72.8 7.1 %copy-start.8 = (f32[8,1024]{1,0:T(8,128)S(1)}, f32[8,1024]{1,0:T(8,128)}, u32[]{:S(2)}) copy-start(f32[8,1024]{1,0:T(8,128)} %get-tuple-element.586) | copy-start | bytes 98308
  72.8 7.1 %copy-start.9 = (f32[8,1024]{1,0:T(8,128)S(1)}, f32[8,1024]{1,0:T(8,128)}, u32[]{:S(2)}) copy-start(f32[8,1024]{1,0:T(8,128)} %get-tuple-element.587) | copy-start | bytes 98308
  88.2 5.8 %collective-permute-start = (bf16[2,8,1024]{2,1,0:T(8,128)(2,1)S(1)}, bf16[2,8,1024]{2,1,0:T(8,128)(2,1)S(1)}, u32[]{:S(2)}, u32[]{:S(2)}) collective-permute-start(bf16[2,8,1024]{2,1,0:T(8,128)(2,1)S(1)} %select_convert_fusion.3), channel_id=1, source_target_pairs={{0,4},{4,8},{8,12},{1,5},{5,9},{9,13},{2,6},{6,10},{10,14},{3,7},{... | collective-permute-start | bytes 98312 | tf_op jit(solution)/shard_map/while/body/eval_jaxpr/ppermute | solution.py:29
  94.0 6.1 %collective-permute-start.1 = (bf16[2,8,1024]{2,1,0:T(8,128)(2,1)S(1)}, bf16[2,8,1024]{2,1,0:T(8,128)(2,1)S(1)}, u32[]{:S(2)}, u32[]{:S(2)}) collective-permute-start(bf16[2,8,1024]{2,1,0:T(8,128)(2,1)S(1)} %collective-permute-done), channel_id=1, source_target_pairs={{2,0},{3,1},{6,4},{7,5},{10,8},{11,9},{14,12},{15,13},{18,16},{19,... | collective-permute-start | bytes 98312 | tf_op jit(solution)/shard_map/while/body/eval_jaxpr/ppermute | solution.py:19
  98.6 5.8 %collective-permute-start.2 = (bf16[2,8,1024]{2,1,0:T(8,128)(2,1)S(1)}, bf16[2,8,1024]{2,1,0:T(8,128)(2,1)S(1)}, u32[]{:S(2)}, u32[]{:S(2)}) collective-permute-start(bf16[2,8,1024]{2,1,0:T(8,128)(2,1)S(1)} %collective-permute-done), channel_id=1, source_target_pairs={{0,2},{1,3},{4,6},{5,7},{8,10},{9,11},{12,14},{13,15},{16,18},{17,... | collective-permute-start | bytes 98312 | tf_op jit(solution)/shard_map/while/body/eval_jaxpr/ppermute | solution.py:17
  108.9 5.8 %collective-permute-start = (bf16[2,8,1024]{2,1,0:T(8,128)(2,1)S(1)}, bf16[2,8,1024]{2,1,0:T(8,128)(2,1)S(1)}, u32[]{:S(2)}, u32[]{:S(2)}) collective-permute-start(bf16[2,8,1024]{2,1,0:T(8,128)(2,1)S(1)} %select_convert_fusion.3), channel_id=1, source_target_pairs={{0,4},{4,8},{8,12},{1,5},{5,9},{9,13},{2,6},{6,10},{10,14},{3,7},{... | collective-permute-start | bytes 98312 | tf_op jit(solution)/shard_map/while/body/eval_jaxpr/ppermute | solution.py:29
  114.7 3.2 %collective-permute-start.1 = (bf16[2,8,1024]{2,1,0:T(8,128)(2,1)S(1)}, bf16[2,8,1024]{2,1,0:T(8,128)(2,1)S(1)}, u32[]{:S(2)}, u32[]{:S(2)}) collective-permute-start(bf16[2,8,1024]{2,1,0:T(8,128)(2,1)S(1)} %collective-permute-done), channel_id=1, source_target_pairs={{2,0},{3,1},{6,4},{7,5},{10,8},{11,9},{14,12},{15,13},{18,16},{19,... | collective-permute-start | bytes 98312 | tf_op jit(solution)/shard_map/while/body/eval_jaxpr/ppermute | solution.py:19
  116.3 5.8 %collective-permute-start.2 = (bf16[2,8,1024]{2,1,0:T(8,128)(2,1)S(1)}, bf16[2,8,1024]{2,1,0:T(8,128)(2,1)S(1)}, u32[]{:S(2)}, u32[]{:S(2)}) collective-permute-start(bf16[2,8,1024]{2,1,0:T(8,128)(2,1)S(1)} %collective-permute-done), channel_id=1, source_target_pairs={{0,2},{1,3},{4,6},{5,7},{8,10},{9,11},{12,14},{13,15},{16,18},{17,... | collective-permute-start | bytes 98312 | tf_op jit(solution)/shard_map/while/body/eval_jaxpr/ppermute | solution.py:17
  126.7 5.8 %collective-permute-start = (bf16[2,8,1024]{2,1,0:T(8,128)(2,1)S(1)}, bf16[2,8,1024]{2,1,0:T(8,128)(2,1)S(1)}, u32[]{:S(2)}, u32[]{:S(2)}) collective-permute-start(bf16[2,8,1024]{2,1,0:T(8,128)(2,1)S(1)} %select_convert_fusion.3), channel_id=1, source_target_pairs={{0,4},{4,8},{8,12},{1,5},{5,9},{9,13},{2,6},{6,10},{10,14},{3,7},{... | collective-permute-start | bytes 98312 | tf_op jit(solution)/shard_map/while/body/eval_jaxpr/ppermute | solution.py:29
  132.5 3.2 %collective-permute-start.1 = (bf16[2,8,1024]{2,1,0:T(8,128)(2,1)S(1)}, bf16[2,8,1024]{2,1,0:T(8,128)(2,1)S(1)}, u32[]{:S(2)}, u32[]{:S(2)}) collective-permute-start(bf16[2,8,1024]{2,1,0:T(8,128)(2,1)S(1)} %collective-permute-done), channel_id=1, source_target_pairs={{2,0},{3,1},{6,4},{7,5},{10,8},{11,9},{14,12},{15,13},{18,16},{19,... | collective-permute-start | bytes 98312 | tf_op jit(solution)/shard_map/while/body/eval_jaxpr/ppermute | solution.py:19
  134.1 5.8 %collective-permute-start.2 = (bf16[2,8,1024]{2,1,0:T(8,128)(2,1)S(1)}, bf16[2,8,1024]{2,1,0:T(8,128)(2,1)S(1)}, u32[]{:S(2)}, u32[]{:S(2)}) collective-permute-start(bf16[2,8,1024]{2,1,0:T(8,128)(2,1)S(1)} %collective-permute-done), channel_id=1, source_target_pairs={{0,2},{1,3},{4,6},{5,7},{8,10},{9,11},{12,14},{13,15},{16,18},{17,... | collective-permute-start | bytes 98312 | tf_op jit(solution)/shard_map/while/body/eval_jaxpr/ppermute | solution.py:17
  144.4 5.8 %collective-permute-start = (bf16[2,8,1024]{2,1,0:T(8,128)(2,1)S(1)}, bf16[2,8,1024]{2,1,0:T(8,128)(2,1)S(1)}, u32[]{:S(2)}, u32[]{:S(2)}) collective-permute-start(bf16[2,8,1024]{2,1,0:T(8,128)(2,1)S(1)} %select_convert_fusion.3), channel_id=1, source_target_pairs={{0,4},{4,8},{8,12},{1,5},{5,9},{9,13},{2,6},{6,10},{10,14},{3,7},{... | collective-permute-start | bytes 98312 | tf_op jit(solution)/shard_map/while/body/eval_jaxpr/ppermute | solution.py:29
  150.2 3.2 %collective-permute-start.1 = (bf16[2,8,1024]{2,1,0:T(8,128)(2,1)S(1)}, bf16[2,8,1024]{2,1,0:T(8,128)(2,1)S(1)}, u32[]{:S(2)}, u32[]{:S(2)}) collective-permute-start(bf16[2,8,1024]{2,1,0:T(8,128)(2,1)S(1)} %collective-permute-done), channel_id=1, source_target_pairs={{2,0},{3,1},{6,4},{7,5},{10,8},{11,9},{14,12},{15,13},{18,16},{19,... | collective-permute-start | bytes 98312 | tf_op jit(solution)/shard_map/while/body/eval_jaxpr/ppermute | solution.py:19
  151.9 5.8 %collective-permute-start.2 = (bf16[2,8,1024]{2,1,0:T(8,128)(2,1)S(1)}, bf16[2,8,1024]{2,1,0:T(8,128)(2,1)S(1)}, u32[]{:S(2)}, u32[]{:S(2)}) collective-permute-start(bf16[2,8,1024]{2,1,0:T(8,128)(2,1)S(1)} %collective-permute-done), channel_id=1, source_target_pairs={{0,2},{1,3},{4,6},{5,7},{8,10},{9,11},{12,14},{13,15},{16,18},{17,... | collective-permute-start | bytes 98312 | tf_op jit(solution)/shard_map/while/body/eval_jaxpr/ppermute | solution.py:17
